TPU v7x, 32 devices: a whole 2x2x4 slice. The times are simulated.
32 devices in a mesh: grp: 2 (over x), src: 16 (over z, y, core).
Axes of the slice: x: 2, y: 2, z: 4, core: 2. Of those that a mesh axis runs over, the one named last changes fastest.
Arguments:
- data_field: bfloat16 [2, 4096, 2048], P(None, ('grp', 'src')), parts along dimension 1, may hold values from -6 to 6
- primary_field: bfloat16 [2, 4096, 2048], P(None, ('grp', 'src')), parts along dimension 1, may hold values from -6 to 6
- station_weight: float32 [2048], replicated, may hold values from 0.25 to 4
- adaptive_filter: float32 [2, 4096], P(None, 'grp'), parts along dimension 1, may hold values from -1 to 1
Outputs:
- demultiple: float32 [2, 4096, 2048], P(None, ('grp', 'src')), parts along dimension 1
There are 2 independent parts, one for each index of `grp`. A program takes and returns all parts, laid end to end along the dimension named above; an argument that names none is the same for every part. Nothing has to cross between parts.
All inputs are finite; a program needn't handle non-finite values.
Results may differ from a plain program's by a relative error of at most 0.008.
Values may be sent and summed in bfloat16 or wider, within the bound.
No kernel may reach another device: no remote copies, remote signals or barrier semaphores. Data moves between devices by JAX's collectives and lax.ppermute only.
A program may use at most 192 MiB of HBM per device.

v0:
```python
import math

import jax
import jax.numpy as jnp
from jax import lax
from jax.sharding import PartitionSpec as P

ORDERS = 12


def blend_rows(field, mirror, left_weight, right_weight):
    top = left_weight[:, None] * field.astype(jnp.float32) + right_weight[None, :] * mirror.astype(
        jnp.float32
    )
    return (top / (left_weight[:, None] + right_weight[None, :])).astype(jnp.bfloat16)


def local(data_field, primary_field, station_weight, adaptive_filter):
    rows = data_field.shape[1]
    order = data_field.shape[2]
    parts = lax.axis_size("src")
    here = lax.axis_index("src")
    received = lax.all_to_all(data_field, "src", split_axis=2, concat_axis=2, tiled=True)
    mirror = received.reshape(2, rows, parts, rows).transpose(0, 3, 2, 1).reshape(2, rows, order)
    own_weight = lax.dynamic_slice_in_dim(station_weight, here * rows, rows)
    local_rows = blend_rows(data_field, mirror, own_weight, station_weight)
    operator = lax.all_gather(local_rows, "src", axis=1, tiled=True)
    factor = 0.8 / math.sqrt(order)
    current = primary_field
    prediction = jnp.zeros(data_field.shape, jnp.float32)
    for step in range(ORDERS):
        stacked = current.reshape(2 * rows, order)
        with_real = jnp.dot(stacked, operator[0], preferred_element_type=jnp.float32)
        with_imag = jnp.dot(stacked, operator[1], preferred_element_type=jnp.float32)
        real_part = (with_real[:rows] - with_imag[rows:]) * factor
        imag_part = (with_imag[:rows] + with_real[rows:]) * factor
        current = jnp.stack([real_part, imag_part]).astype(jnp.bfloat16)
        prediction = prediction + current.astype(jnp.float32)
    filt_re = adaptive_filter[0][None, :]
    filt_im = adaptive_filter[1][None, :]
    out_re = data_field[0].astype(jnp.float32) - (filt_re * prediction[0] - filt_im * prediction[1])
    out_im = data_field[1].astype(jnp.float32) - (filt_re * prediction[1] + filt_im * prediction[0])
    return jnp.stack([out_re, out_im])


def solution(mesh):
    return jax.shard_map(
        local,
        mesh=mesh,
        in_specs=(
            P(None, ("grp", "src"), None),
            P(None, ("grp", "src"), None),
            P(),
            P(None, "grp"),
        ),
        out_specs=P(None, ("grp", "src"), None),
        check_vma=False,
    )
```

profile of v0, /device:TPU:0, one launch (start us, length us, event | category | flops | bytes accessed | tf_op | source)
XLA Modules:
  0.0 261.7 jit_solution(17887234792733334002)
XLA Ops:
  6.5 3.8 %copy.6 = bf16[2,128,2048]{1,0,2:T(2,128)(2,1)} copy(bf16[2,128,2048]{2,1,0:T(8,128)(2,1)} %param.4) | data formatting | bytes 2097152 | tf_op args[0]
  10.3 7.4 %all-to-all-start = ((bf16[2,128,2048]{1,0,2:T(2,128)(2,1)}), bf16[2,128,2048]{1,0,2:T(2,128)(2,1)S(1)}, u32[]{:S(2)}, u32[]{:S(2)}) async-start(bf16[2,128,2048]{1,0,2:T(2,128)(2,1)} %copy.6), calls=%async_computation | async-start | bytes 2097152 | tf_op jit(solution)/shard_map/all_to_all | solution.py:23
  18.0 22.6 %all-to-all-done = bf16[2,128,2048]{1,0,2:T(2,128)(2,1)S(1)} async-done(((bf16[2,128,2048]{1,0,2:T(2,128)(2,1)}), bf16[2,128,2048]{1,0,2:T(2,128)(2,1)S(1)}, u32[]{:S(2)}, u32[]{:S(2)}) %all-to-all-start) | async-done | bytes 1048608 | tf_op jit(solution)/shard_map/all_to_all | solution.py:23
  41.5 2.5 copy.7
  44.0 3.3 %reshape.206 = f32[2,128,2048]{2,1,0:T(8,128)} reshape(f32[2,128,16,128]{3,2,1,0:T(8,128)} %copy.7) | data formatting | bytes 4194304 | tf_op jit(solution)/shard_map/convert_element_type | solution.py:12
  47.3 3.1 %divide_convert_fusion = bf16[2,128,2048]{2,1,0:T(8,128)(2,1)} fusion(f32[2,128,2048]{2,1,0:T(8,128)} %reshape.206, bf16[2,128,2048]{2,1,0:T(8,128)(2,1)S(1)} %copy-done.2, f32[128,2048]{1,0:T(8,128)S(1)} %broadcast_add_fusion, f32[2048]{0:T(1024)S(1)} %copy-done.3, f32[128]{0:T(128)S(1)} %dynamic_slice.3), kind=kLoop, calls=%fused_computation.7 | loop fusion | flops 3145728 | bytes 5251584 | tf_op jit(solution)/shard_map/convert_element_type | solution.py:15
  50.5 128.7 %all-gather.2.cloned.1.call-done = bf16[2,2048,2048]{2,1,0:T(8,128)(2,1)} async-done(((bf16[2,128,2048]{2,1,0:T(8,128)(2,1)}), bf16[2,2048,2048]{2,1,0:T(8,128)(2,1)}) %all-gather.2.cloned.1.call-update) | async-done | bytes 16777232 | tf_op jit(solution)/shard_map/all_gather | solution.py:27
  179.2 5.9 %convolution_bitcast_fusion = f32[256,2048]{1,0:T(8,128)S(1)} fusion(bf16[256,2048]{1,0:T(8,128)(2,1)S(1)} %bitcast.124, bf16[2,2048,2048]{2,1,0:T(8,128)(2,1)} %all-gather.2.cloned.1.call-done), kind=kOutput, calls=%fused_computation.2 | convolution fusion | flops 2147483648 | bytes 11534336 | tf_op jit(solution)/shard_map/dot_general | solution.py:34
  185.1 5.9 %convolution_bitcast_fusion.1 = f32[256,2048]{1,0:T(8,128)S(1)} fusion(bf16[256,2048]{1,0:T(8,128)(2,1)S(1)} %bitcast.125, bf16[2,2048,2048]{2,1,0:T(8,128)(2,1)} %all-gather.2.cloned.1.call-done), kind=kOutput, calls=%fused_computation.3 | convolution fusion | flops 2147483648 | bytes 11534336 | tf_op jit(solution)/shard_map/dot_general | solution.py:33
  191.5 2.4 fusion.82
  193.9 2.4 fusion.93
  199.3 2.4 fusion.92
  204.8 2.4 fusion.91
  210.1 2.4 fusion.90
  215.4 2.4 fusion.89
  218.3 2.6 %fusion.77 = f32[256,2048]{1,0:T(8,128)S(1)} fusion(bf16[256,2048]{1,0:T(8,128)(2,1)S(1)} %bitcast.139, bf16[2,2048,2048]{2,1,0:T(8,128)(2,1)S(1)} %bitcast.152), kind=kOutput, calls=%fused_computation.123 | convolution fusion | flops 2147483648 | bytes 11534336 | tf_op jit(solution)/shard_map/dot_general | solution.py:33
  221.0 2.4 fusion.88
  226.3 2.4 fusion.87
  229.2 2.4 fusion.75
  231.6 2.4 fusion.86
  234.5 2.8 %fusion.74 = f32[256,2048]{1,0:T(8,128)S(1)} fusion(bf16[256,2048]{1,0:T(8,128)(2,1)S(1)} %bitcast.145, bf16[2,2048,2048]{2,1,0:T(8,128)(2,1)S(1)} %bitcast.152), kind=kOutput, calls=%fused_computation.120 | convolution fusion | flops 2147483648 | bytes 11534336 | tf_op jit(solution)/shard_map/dot_general | solution.py:33
  237.4 2.4 fusion.85
  242.7 2.4 fusion.84
  245.6 2.4 fusion.72
  (58 shorter events, 28.1 us)
Async XLA Ops:
  6.5 172.7 %copy-start = (bf16[2,128,2048]{2,1,0:T(8,128)(2,1)S(1)}, bf16[2,128,2048]{2,1,0:T(8,128)(2,1)}, u32[]{:S(2)}) copy-start(bf16[2,128,2048]{2,1,0:T(8,128)(2,1)} %param.5) | copy-start | bytes 3145732
  6.5 11.2 %copy-start.3 = (f32[2048]{0:T(1024)S(1)}, f32[2048]{0:T(1024)}, u32[]{:S(2)}) copy-start(f32[2048]{0:T(1024)} %param.6) | copy-start | bytes 24580
  10.3 30.3 %all-to-all-start = ((bf16[2,128,2048]{1,0,2:T(2,128)(2,1)}), bf16[2,128,2048]{1,0,2:T(2,128)(2,1)S(1)}, u32[]{:S(2)}, u32[]{:S(2)}) async-start(bf16[2,128,2048]{1,0,2:T(2,128)(2,1)} %copy.6), calls=%async_computation | async-start | bytes 2097152 | tf_op jit(solution)/shard_map/all_to_all | solution.py:23
  17.7 161.5 %all-gather.2.cloned.1.call-start = ((), (), s32[]{:S(2)}) async-start(), calls=%async_computation.1 | async-start | bytes 17825792 | tf_op jit(solution)/shard_map/all_gather | solution.py:27
  44.0 3.3 %copy-start.2 = (bf16[2,128,2048]{2,1,0:T(8,128)(2,1)S(1)}, bf16[2,128,2048]{2,1,0:T(8,128)(2,1)}, u32[]{:S(2)}) copy-start(bf16[2,128,2048]{2,1,0:T(8,128)(2,1)} %param.4) | copy-start | bytes 3145732
  47.3 3.1 %copy-start.4 = (f32[2,2048]{1,0:T(2,128)S(1)}, f32[2,2048]{1,0:T(2,128)}, u32[]{:S(2)}) copy-start(f32[2,2048]{1,0:T(2,128)} %param.7) | copy-start | bytes 49156
  179.2 12.3 %slice-start = ((s8[16777216]{0:T(1024)(128)(4,1)}), s8[4194304]{0:T(1024)(128)(4,1)S(1)}, s32[]{:S(2)}) async-start(s8[16777216]{0:T(1024)(128)(4,1)} %bitcast.151), calls=%async_computation.2 | async-start | bytes 8388608
  179.2 12.3 %slice-start.1 = ((s8[16777216]{0:T(1024)(128)(4,1)}), s8[4194304]{0:T(1024)(128)(4,1)S(1)}, s32[]{:S(2)}) async-start(s8[16777216]{0:T(1024)(128)(4,1)} %bitcast.151), calls=%async_computation.3 | async-start | bytes 8388608
  185.1 6.4 %slice-start.2 = ((s8[16777216]{0:T(1024)(128)(4,1)}), s8[4194304]{0:T(1024)(128)(4,1)S(1)}, s32[]{:S(2)}) async-start(s8[16777216]{0:T(1024)(128)(4,1)} %bitcast.151), calls=%async_computation.4 | async-start | bytes 8388608
  185.1 6.4 %slice-start.3 = ((s8[16777216]{0:T(1024)(128)(4,1)}), s8[4194304]{0:T(1024)(128)(4,1)S(1)}, s32[]{:S(2)}) async-start(s8[16777216]{0:T(1024)(128)(4,1)} %bitcast.151), calls=%async_computation.5 | async-start | bytes 8388608
  253.1 1.6 copy-start.1
Sparse Core Ops, SparseCore 0:
  50.6 128.5 all-gather.1
where the time goes:
time: 265 us; the launch traced here: 262 us
  waiting for transfers between devices  151 us (57%)
  matrix products  64.9 us (24%)
  other arithmetic  14.2 us (5%)
  between operations  14.1 us (5%)
  local copies, waits for them, and re-layouts  9.79 us (4%)
  starting transfers between devices  7.45 us (3%)
    all_gather x1, waiting for transfers between devices, local(): operator = lax.all_gather(local_rows, 'src', axis=1, tiled=True)  129 us
    dot_general x12, matrix products, local(): jnp.dot(stacked, operator[0], preferred_element_type=jnp.float32)  32.8 us
    dot_general x12, matrix products, local(): jnp.dot(stacked, operator[1], preferred_element_type=jnp.float32)  32.1 us
    all_to_all x1, waiting for transfers between devices, local(): lax.all_to_all(data_field, 'src', split_axis=2, concat_axis=2, tiled=True)  22.6 us
    all_to_all x1, starting transfers between devices, local(): lax.all_to_all(data_field, 'src', split_axis=2, concat_axis=2, tiled=True)  7.41 us
    another operation x23, other arithmetic, local(): current = jnp.stack([real_part, imag_part]).astype(jnp.bfloat16)  6.31 us
    convert_element_type x2, local copies, waits for them, and re-layouts, blend_rows(): mirror.astype(jnp.float32)  5.8 us
  transfers between devices with their start and end apart: 2, of which 2 were waited for; matrix products, arithmetic and copies ran while one was open for 0% of the time, Pallas kernels for 0%

commit v1 on v0

--- a/solution.py
+++ b/solution.py
@@ -1,11 +1,13 @@
 import math
 
+import numpy as np
 import jax
 import jax.numpy as jnp
 from jax import lax
-from jax.sharding import PartitionSpec as P
+from jax.sharding import Mesh, PartitionSpec as P
 
 ORDERS = 12
+AXES = ("chip", "core")
 
 
 def blend_rows(field, mirror, left_weight, right_weight):
@@ -15,16 +17,54 @@
     return (top / (left_weight[:, None] + right_weight[None, :])).astype(jnp.bfloat16)
 
 
+def upper_blocks(data_field, station_weight, parts, here):
+    rows = data_field.shape[1]
+    own_weight = lax.dynamic_slice_in_dim(station_weight, here * rows, rows)
+    blocks = []
+    for s in range(parts // 2 + 1):
+        col = ((here + s) % parts) * rows
+        own = lax.dynamic_slice_in_dim(data_field, col, rows, axis=2)
+        if s == 0:
+            mirror = own.swapaxes(1, 2)
+        else:
+            send = lax.dynamic_slice_in_dim(data_field, ((here - s) % parts) * rows, rows, axis=2)
+            recv = lax.ppermute(send, AXES, perm=[(c, (c - s) % parts) for c in range(parts)])
+            mirror = recv.swapaxes(1, 2)
+        col_weight = lax.dynamic_slice_in_dim(station_weight, col, rows)
+        blocks.append(blend_rows(own, mirror, own_weight, col_weight))
+    return jnp.stack(blocks)
+
+
+def assemble(gathered, chips, cores):
+    parts = chips * cores
+    slots = gathered.shape[2]
+    rows = gathered.shape[-1]
+    flat = gathered.reshape((parts, slots) + gathered.shape[3:])
+    both = jnp.concatenate([flat, flat.swapaxes(-1, -2)], axis=1)
+    where = lambda a: (a % cores) * chips + a // cores
+    idx_a = np.zeros((parts, parts), np.int32)
+    idx_s = np.zeros((parts, parts), np.int32)
+    for r in range(parts):
+        for c in range(parts):
+            s = (c - r) % parts
+            if s <= parts // 2:
+                idx_a[r, c], idx_s[r, c] = where(r), s
+            else:
+                idx_a[r, c], idx_s[r, c] = where(c), slots + (r - c) % parts
+    blocks = both[idx_a, idx_s]
+    return blocks.transpose(2, 0, 3, 1, 4).reshape(2, parts * rows, parts * rows)
+
+
 def local(data_field, primary_field, station_weight, adaptive_filter):
     rows = data_field.shape[1]
     order = data_field.shape[2]
-    parts = lax.axis_size("src")
-    here = lax.axis_index("src")
-    received = lax.all_to_all(data_field, "src", split_axis=2, concat_axis=2, tiled=True)
-    mirror = received.reshape(2, rows, parts, rows).transpose(0, 3, 2, 1).reshape(2, rows, order)
-    own_weight = lax.dynamic_slice_in_dim(station_weight, here * rows, rows)
-    local_rows = blend_rows(data_field, mirror, own_weight, station_weight)
-    operator = lax.all_gather(local_rows, "src", axis=1, tiled=True)
+    chips = lax.axis_size("chip")
+    cores = lax.axis_size("core")
+    parts = chips * cores
+    here = lax.axis_index("chip") * cores + lax.axis_index("core")
+    mine = upper_blocks(data_field, station_weight, parts, here)
+    gathered = lax.all_gather(lax.all_gather(mine, "chip"), "core")
+    operator = assemble(gathered, chips, cores)
     factor = 0.8 / math.sqrt(order)
     current = primary_field
     prediction = jnp.zeros(data_field.shape, jnp.float32)
@@ -44,15 +84,13 @@
 
 
 def solution(mesh):
+    groups, parts = mesh.devices.shape
+    split = Mesh(mesh.devices.reshape(groups, parts // 2, 2), ("grp",) + AXES)
+    rows_spec = P(None, ("grp",) + AXES, None)
     return jax.shard_map(
         local,
-        mesh=mesh,
-        in_specs=(
-            P(None, ("grp", "src"), None),
-            P(None, ("grp", "src"), None),
-            P(),
-            P(None, "grp"),
-        ),
-        out_specs=P(None, ("grp", "src"), None),
+        mesh=split,
+        in_specs=(rows_spec, rows_spec, P(), P(None, "grp")),
+        out_specs=rows_spec,
         check_vma=False,
     )

time: 265 us -> 303 us (1.14)
  local copies, waits for them, and re-layouts: 9.79 us -> 74.9 us
  waiting for transfers between devices: 151 us -> 101 us
  other arithmetic: 14.2 us -> 33.4 us
  starting transfers between devices: 7.45 us -> 13.1 us
  matrix products: 64.9 us -> 60.9 us
    slice x0 -> x3, local copies, waits for them, and re-layouts: none -> 39.8 us  [the longest x2 26.1 us: local(): operator[1]]
    all_gather x1 -> x2, waiting for transfers between devices: 129 us -> 100 us  [local(): gathered = lax.all_gather(lax.all_gather(mine, 'chip'), 'core')]
    all_to_all x1 -> x0, waiting for transfers between devices: 22.6 us -> none  [local(): lax.all_to_all(data_field, 'src', split_axis=2, concat_axis=2, tiled=True)]
    gather x0 -> x1, local copies, waits for them, and re-layouts: none -> 17.4 us  [assemble(): blocks = both[idx_a, idx_s]]
    concatenate x0 -> x1, other arithmetic: none -> 15 us  [assemble(): both = jnp.concatenate([flat, flat.swapaxes(-1, -2)], axis=1)]
    ppermute x0 -> x8, starting transfers between devices: none -> 13.1 us  [upper_blocks(): lax.ppermute(send, AXES, perm=[(c, (c - s) % parts) for c in range(parts)])]
    all_gather x0 -> x1, local copies, waits for them, and re-layouts: none -> 12.7 us  [local(): gathered = lax.all_gather(lax.all_gather(mine, 'chip'), 'core')]
    all_to_all x1 -> x0, starting transfers between devices: 7.41 us -> none  [local(): lax.all_to_all(data_field, 'src', split_axis=2, concat_axis=2, tiled=True)]
  transfers between devices with their start and end apart: 2 -> 10, of which waited for: 2 -> 3; matrix products, arithmetic and copies ran while one was open for 0% -> 3% of each run, Pallas kernels for 0% -> 0%
where the time goes in v1:
time: 303 us; the launch traced here: 298 us
  waiting for transfers between devices  101 us (33%)
  local copies, waits for them, and re-layouts  74.9 us (25%)
  matrix products  60.9 us (20%)
  other arithmetic  33.4 us (11%)
  between operations  14.3 us (5%)
  starting transfers between devices  13.1 us (4%)
    all_gather x2, waiting for transfers between devices, local(): gathered = lax.all_gather(lax.all_gather(mine, 'chip'), 'core')  100 us
    dot_general x12, matrix products, local(): jnp.dot(stacked, operator[0], preferred_element_type=jnp.float32)  32.2 us
    dot_general x12, matrix products, local(): jnp.dot(stacked, operator[1], preferred_element_type=jnp.float32)  28.7 us
    slice x2, local copies, waits for them, and re-layouts, local(): operator[1]  26.1 us
    gather x1, local copies, waits for them, and re-layouts, assemble(): blocks = both[idx_a, idx_s]  17.4 us
    concatenate x1, other arithmetic, assemble(): both = jnp.concatenate([flat, flat.swapaxes(-1, -2)], axis=1)  15 us
    slice x1, local copies, waits for them, and re-layouts, local(): operator[0]  13.7 us
    ppermute x8, starting transfers between devices, upper_blocks(): lax.ppermute(send, AXES, perm=[(c, (c - s) % parts) for c in range(parts)])  13.1 us
  transfers between devices with their start and end apart: 10, of which 3 were waited for; matrix products, arithmetic and copies ran while one was open for 3% of the time, Pallas kernels for 0%

profile of v1, /device:TPU:0, one launch (start us, length us, event | category | flops | bytes accessed | tf_op | source)
XLA Modules:
  0.0 297.7 jit_solution(7573258853512313184)
XLA Ops:
  7.9 5.5 %collective-permute-start = (bf16[2,128,128]{1,2,0:T(8,128)(2,1)S(1)}, bf16[2,128,128]{1,2,0:T(8,128)(2,1)S(1)}, u32[]{:S(2)}, u32[]{:S(2)}) collective-permute-start(bf16[2,128,128]{1,2,0:T(8,128)(2,1)S(1)} %copy.72), channel_id=1, source_target_pairs={{0,15},{1,0},{2,1},{3,2},{4,3},{5,4},{6,5},{7,6},{8,7},{9,8},{10,9... | collective-permute-start | bytes 196616 | tf_op jit(solution)/shard_map/ppermute | solution.py:31
  17.6 4.3 %collective-permute-start.5 = (bf16[2,128,128]{1,2,0:T(8,128)(2,1)S(1)}, bf16[2,128,128]{1,2,0:T(8,128)(2,1)S(1)}, u32[]{:S(2)}, u32[]{:S(2)}) collective-permute-start(bf16[2,128,128]{1,2,0:T(8,128)(2,1)S(1)} %copy.77), channel_id=1, source_target_pairs={{0,10},{1,11},{2,12},{3,13},{4,14},{5,15},{6,0},{7,1},{8,2},{9,3},... | collective-permute-start | bytes 196616 | tf_op jit(solution)/shard_map/ppermute | solution.py:31
  32.9 79.3 %all-gather.5.cloned.1.call-done = bf16[72,2,128,128]{3,2,1,0:T(8,128)(2,1)} async-done(((bf16[9,2,128,128]{3,2,1,0:T(8,128)(2,1)}), bf16[72,2,128,128]{3,2,1,0:T(8,128)(2,1)}) %all-gather.5.cloned.1.call-update) | async-done | bytes 4718608 | tf_op jit(solution)/shard_map/all_gather | solution.py:66
  112.9 20.9 %all-gather.7.cloned.1.call-done = bf16[16,9,2,128,128]{4,3,2,1,0:T(8,128)(2,1)} async-done(((bf16[8,9,2,128,128]{4,3,2,1,0:T(8,128)(2,1)}), bf16[16,9,2,128,128]{4,3,2,1,0:T(8,128)(2,1)}) %all-gather.7.cloned.1.call-update) | async-done | bytes 9437200 | tf_op jit(solution)/shard_map/all_gather | solution.py:66
  133.8 12.7 %copy.68 = bf16[16,9,2,128,128]{3,4,2,1,0:T(8,128)(2,1)} copy(bf16[16,9,2,128,128]{4,3,2,1,0:T(8,128)(2,1)} %all-gather.7.cloned.1.call-done) | data formatting | bytes 18874368 | tf_op jit(solution)/shard_map/all_gather | solution.py:66
  146.5 15.0 %pad_maximum_fusion = bf16[16,18,2,128,128]{4,3,2,1,0:T(8,128)(2,1)} fusion(bf16[16,9,2,128,128]{4,3,2,1,0:T(8,128)(2,1)} %bitcast.246, bf16[16,9,2,128,128]{4,3,2,1,0:T(8,128)(2,1)} %all-gather.7.cloned.1.call-done), kind=kLoop, calls=%fused_computation.1 | loop fusion | flops 9437184 | bytes 37748736 | tf_op jit(solution)/shard_map/concatenate | solution.py:43
  161.5 17.4 %gather_fusion = bf16[256,2,128,128]{3,2,1,0:T(8,128)(2,1)} fusion(bf16[16,18,2,128,128]{4,3,2,1,0:T(8,128)(2,1)} %pad_maximum_fusion, s32[256]{0:T(256)S(1)} %copy-done.2), kind=kCustom, calls=%fused_computation | custom fusion | bytes 33556480 | tf_op jit(solution)/shard_map/gather | solution.py:54
  178.9 12.1 %fusion.168 = (bf16[1,16,128,16,128]{4,2,0,3,1:T(8,128)(2,1)}, bf16[1,16,128,16,128]{4,2,0,3,1:T(8,128)(2,1)}) fusion(bf16[2,16,128,16,128]{4,2,0,3,1:T(8,128)(2,1)} %bitcast.245), kind=kLoop, calls=%fused_computation.241 | loop fusion | bytes 33554432 | tf_op jit(solution)/shard_map/slice | solution.py:74
  191.0 13.7 %copy.69 = bf16[1,16,128,16,128]{4,3,2,1,0:T(8,128)(2,1)} copy(bf16[1,16,128,16,128]{4,2,0,3,1:T(8,128)(2,1)} %get-tuple-element.6) | data formatting | bytes 16777216 | tf_op jit(solution)/shard_map/slice | solution.py:73
  204.7 13.9 %copy.70 = bf16[1,16,128,16,128]{4,3,2,1,0:T(8,128)(2,1)} copy(bf16[1,16,128,16,128]{4,2,0,3,1:T(8,128)(2,1)} %get-tuple-element.5) | data formatting | bytes 16777216 | tf_op jit(solution)/shard_map/slice | solution.py:74
  218.7 5.9 %fusion.48 = f32[256,2048]{1,0:T(8,128)S(1)} fusion(bf16[256,2048]{1,0:T(8,128)(2,1)S(1)} %bitcast.244, bf16[256,8,16,128]{3,2,1,0:T(8,128)(2,1)} %bitcast.247), kind=kOutput, calls=%fused_computation.50 | convolution fusion | flops 2147483648 | bytes 11534336 | tf_op jit(solution)/shard_map/dot_general | solution.py:73
  224.6 2.4 fusion.51
  229.9 2.4 fusion.20
  233.3 2.4 fusion.42
  235.6 2.4 fusion.18
  238.6 2.4 fusion.40
  243.9 2.5 fusion.38
  251.7 2.4 fusion.12
  254.6 2.4 fusion.34
  257.0 2.4 fusion.10
  268.0 2.4 fusion.6
  273.3 2.6 fusion.4
  278.8 2.4 fusion.2
  284.1 2.4 fusion
  (100 shorter events, 51.3 us)
Async XLA Ops:
  6.5 212.1 %copy-start = (bf16[2,128,2048]{2,1,0:T(8,128)(2,1)S(1)}, bf16[2,128,2048]{2,1,0:T(8,128)(2,1)}, u32[]{:S(2)}) copy-start(bf16[2,128,2048]{2,1,0:T(8,128)(2,1)} %param.9) | copy-start | bytes 3145732
  6.5 105.7 %copy-start.8 = (f32[2,2048]{1,0:T(2,128)S(1)}, f32[2,2048]{1,0:T(2,128)}, u32[]{:S(2)}) copy-start(f32[2,2048]{1,0:T(2,128)} %param.11) | copy-start | bytes 49156
  6.5 105.7 %all-gather.5.cloned.1.call-start = ((), (), s32[]{:S(2)}) async-start(), calls=%async_computation | async-start | bytes 5308416 | tf_op jit(solution)/shard_map/all_gather | solution.py:66
  7.9 9.7 %collective-permute-start = (bf16[2,128,128]{1,2,0:T(8,128)(2,1)S(1)}, bf16[2,128,128]{1,2,0:T(8,128)(2,1)S(1)}, u32[]{:S(2)}, u32[]{:S(2)}) collective-permute-start(bf16[2,128,128]{1,2,0:T(8,128)(2,1)S(1)} %copy.72), channel_id=1, source_target_pairs={{0,15},{1,0},{2,1},{3,2},{4,3},{5,4},{6,5},{7,6},{8,7},{9,8},{10,9... | collective-permute-start | bytes 196616 | tf_op jit(solution)/shard_map/ppermute | solution.py:31
  13.6 9.3 %collective-permute-start.1 = (bf16[2,128,128]{1,2,0:T(8,128)(2,1)S(1)}, bf16[2,128,128]{1,2,0:T(8,128)(2,1)S(1)}, u32[]{:S(2)}, u32[]{:S(2)}) collective-permute-start(bf16[2,128,128]{1,2,0:T(8,128)(2,1)S(1)} %copy.73), channel_id=1, source_target_pairs={{0,14},{1,15},{2,0},{3,1},{4,2},{5,3},{6,4},{7,5},{8,6},{9,7},{10,... | collective-permute-start | bytes 196616 | tf_op jit(solution)/shard_map/ppermute | solution.py:31
  14.3 9.6 %collective-permute-start.2 = (bf16[2,128,128]{1,2,0:T(8,128)(2,1)S(1)}, bf16[2,128,128]{1,2,0:T(8,128)(2,1)S(1)}, u32[]{:S(2)}, u32[]{:S(2)}) collective-permute-start(bf16[2,128,128]{1,2,0:T(8,128)(2,1)S(1)} %copy.74), channel_id=1, source_target_pairs={{0,13},{1,14},{2,15},{3,0},{4,1},{5,2},{6,3},{7,4},{8,5},{9,6},{10... | collective-permute-start | bytes 196616 | tf_op jit(solution)/shard_map/ppermute | solution.py:31
  14.8 11.7 %collective-permute-start.3 = (bf16[2,128,128]{1,2,0:T(8,128)(2,1)S(1)}, bf16[2,128,128]{1,2,0:T(8,128)(2,1)S(1)}, u32[]{:S(2)}, u32[]{:S(2)}) collective-permute-start(bf16[2,128,128]{1,2,0:T(8,128)(2,1)S(1)} %copy.75), channel_id=1, source_target_pairs={{0,12},{1,13},{2,14},{3,15},{4,0},{5,1},{6,2},{7,3},{8,4},{9,5},{1... | collective-permute-start | bytes 196616 | tf_op jit(solution)/shard_map/ppermute | solution.py:31
  15.4 12.0 %collective-permute-start.4 = (bf16[2,128,128]{1,2,0:T(8,128)(2,1)S(1)}, bf16[2,128,128]{1,2,0:T(8,128)(2,1)S(1)}, u32[]{:S(2)}, u32[]{:S(2)}) collective-permute-start(bf16[2,128,128]{1,2,0:T(8,128)(2,1)S(1)} %copy.76), channel_id=1, source_target_pairs={{0,11},{1,12},{2,13},{3,14},{4,15},{5,0},{6,1},{7,2},{8,3},{9,4},{... | collective-permute-start | bytes 196616 | tf_op jit(solution)/shard_map/ppermute | solution.py:31
  17.6 10.8 %collective-permute-start.5 = (bf16[2,128,128]{1,2,0:T(8,128)(2,1)S(1)}, bf16[2,128,128]{1,2,0:T(8,128)(2,1)S(1)}, u32[]{:S(2)}, u32[]{:S(2)}) collective-permute-start(bf16[2,128,128]{1,2,0:T(8,128)(2,1)S(1)} %copy.77), channel_id=1, source_target_pairs={{0,10},{1,11},{2,12},{3,13},{4,14},{5,15},{6,0},{7,1},{8,2},{9,3},... | collective-permute-start | bytes 196616 | tf_op jit(solution)/shard_map/ppermute | solution.py:31
  22.9 6.5 %collective-permute-start.6 = (bf16[2,128,128]{1,2,0:T(8,128)(2,1)S(1)}, bf16[2,128,128]{1,2,0:T(8,128)(2,1)S(1)}, u32[]{:S(2)}, u32[]{:S(2)}) collective-permute-start(bf16[2,128,128]{1,2,0:T(8,128)(2,1)S(1)} %copy.78), channel_id=1, source_target_pairs={{0,9},{1,10},{2,11},{3,12},{4,13},{5,14},{6,15},{7,0},{8,1},{9,2},... | collective-permute-start | bytes 196616 | tf_op jit(solution)/shard_map/ppermute | solution.py:31
  23.9 7.2 %collective-permute-start.7 = (bf16[2,128,128]{1,2,0:T(8,128)(2,1)S(1)}, bf16[2,128,128]{1,2,0:T(8,128)(2,1)S(1)}, u32[]{:S(2)}, u32[]{:S(2)}) collective-permute-start(bf16[2,128,128]{1,2,0:T(8,128)(2,1)S(1)} %copy.79), channel_id=1, source_target_pairs={{0,8},{1,9},{2,10},{3,11},{4,12},{5,13},{6,14},{7,15},{8,0},{9,1},... | collective-permute-start | bytes 196616 | tf_op jit(solution)/shard_map/ppermute | solution.py:31
  32.0 0.8 copy-start.5
  32.9 101.0 %all-gather.7.cloned.1.call-start = ((), (), s32[]{:S(2)}) async-start(), calls=%async_computation.1 | async-start | bytes 14155776 | tf_op jit(solution)/shard_map/all_gather | solution.py:66
  146.5 15.0 %copy-start.2 = (s32[256]{0:T(256)S(1)}, s32[256]{0:T(256)}, u32[]{:S(2)}) copy-start(s32[256]{0:T(256)} %constant.159) | copy-start | bytes 3076
  218.7 5.9 %copy-start.3 = (bf16[1,16,128,16,128]{4,3,2,1,0:T(8,128)(2,1)S(1)}, bf16[1,16,128,16,128]{4,3,2,1,0:T(8,128)(2,1)}, u32[]{:S(2)}) copy-start(bf16[1,16,128,16,128]{4,3,2,1,0:T(8,128)(2,1)} %copy.70) | copy-start | bytes 25165828
  218.7 8.9 %slice-start = ((s8[8388608]{0:T(1024)(128)(4,1)}), s8[4194304]{0:T(1024)(128)(4,1)S(1)}, s32[]{:S(2)}) async-start(s8[8388608]{0:T(1024)(128)(4,1)} %bitcast.248), calls=%async_computation.2 | async-start | bytes 8388608
  224.6 3.0 slice-start.1
  286.9 2.0 copy-start.4
  286.9 1.9 copy-start.6
  286.9 1.9 copy-start.7
  286.9 3.8 %copy-start.1 = (bf16[2,128,2048]{2,1,0:T(8,128)(2,1)S(1)}, bf16[2,128,2048]{2,1,0:T(8,128)(2,1)}, u32[]{:S(2)}) copy-start(bf16[2,128,2048]{2,1,0:T(8,128)(2,1)} %param.9) | copy-start | bytes 3145732
Sparse Core Ops, SparseCore 0:
  33.0 79.2 all-gather.4
  113.8 19.9 all-gather.6

commit v2 on v1

--- a/solution.py
+++ b/solution.py
@@ -4,6 +4,8 @@
 import jax
 import jax.numpy as jnp
 from jax import lax
+from jax.experimental import pallas as pl
+from jax.experimental.pallas import tpu as pltpu
 from jax.sharding import Mesh, PartitionSpec as P
 
 ORDERS = 12
@@ -55,6 +57,49 @@
     return blocks.transpose(2, 0, 3, 1, 4).reshape(2, parts * rows, parts * rows)
 
 
+def assemble_kernel(g_ref, re_ref, im_ref, buf, sem):
+    cores, chips, slots, _, rows, _ = g_ref.shape
+    parts = chips * cores
+    r = pl.program_id(0)
+    copies = []
+    for c in range(parts):
+        s = (c - r + parts) % parts
+        up = s <= parts // 2
+        a = jnp.where(up, r, c)
+        src = g_ref.at[a % cores, a // cores, jnp.where(up, s, parts - s)]
+        copy = pltpu.make_async_copy(src, buf.at[c], sem.at[c])
+        copy.start()
+        copies.append(copy)
+    for c in range(parts):
+        copies[c].wait()
+        s = (c - r + parts) % parts
+        up = s <= parts // 2
+        for k, out in ((0, re_ref), (1, im_ref)):
+            block = buf[c, k]
+
+            @pl.when(up)
+            def _():
+                out[:, c * rows:(c + 1) * rows] = block
+
+            @pl.when(jnp.logical_not(up))
+            def _():
+                out[:, c * rows:(c + 1) * rows] = block.astype(jnp.float32).T.astype(jnp.bfloat16)
+
+
+def assemble_pallas(gathered, chips, cores):
+    parts = chips * cores
+    rows = gathered.shape[-1]
+    order = parts * rows
+    return pl.pallas_call(
+        assemble_kernel,
+        grid=(parts,),
+        in_specs=[pl.BlockSpec(memory_space=pl.ANY)],
+        out_specs=[pl.BlockSpec((rows, order), lambda r: (r, 0))] * 2,
+        out_shape=[jax.ShapeDtypeStruct((order, order), jnp.bfloat16)] * 2,
+        scratch_shapes=[pltpu.VMEM((parts, 2, rows, rows), jnp.bfloat16), pltpu.SemaphoreType.DMA((parts,))],
+    )(gathered)
+
+
 def local(data_field, primary_field, station_weight, adaptive_filter):
     rows = data_field.shape[1]
     order = data_field.shape[2]
@@ -64,7 +109,10 @@
     here = lax.axis_index("chip") * cores + lax.axis_index("core")
     mine = upper_blocks(data_field, station_weight, parts, here)
     gathered = lax.all_gather(lax.all_gather(mine, "chip"), "core")
-    operator = assemble(gathered, chips, cores)
+    if rows % 128 == 0:
+        operator = assemble_pallas(gathered, chips, cores)
+    else:
+        operator = assemble(gathered, chips, cores)
     factor = 0.8 / math.sqrt(order)
     current = primary_field
     prediction = jnp.zeros(data_field.shape, jnp.float32)

time: 303 us -> 270 us (0.89)
  local copies, waits for them, and re-layouts: 74.9 us -> 10.2 us
  Pallas kernels: 0 us -> 46.8 us
  other arithmetic: 33.4 us -> 15.8 us
    pallas_call x0 -> x1, Pallas kernels: none -> 46.8 us  [assemble_pallas(): pl.pallas_call(assemble_kernel, grid=(parts,), in_specs=[pl.BlockSpec(mem...]
    slice x3 -> x0, local copies, waits for them, and re-layouts: 39.8 us -> none  [the longest x2 26.1 us: local(): operator[1]]
    gather x1 -> x0, local copies, waits for them, and re-layouts: 17.4 us -> none  [assemble(): blocks = both[idx_a, idx_s]]
    concatenate x1 -> x0, other arithmetic: 15 us -> none  [assemble(): both = jnp.concatenate([flat, flat.swapaxes(-1, -2)], axis=1)]
    all_gather x1 -> x0, local copies, waits for them, and re-layouts: 12.7 us -> none  [local(): gathered = lax.all_gather(lax.all_gather(mine, 'chip'), 'core')]
    unnamed x31 -> x51, local copies, waits for them, and re-layouts: 1.94 us -> 8.23 us
    dot_general x12, matrix products: 28.7 us -> 32.2 us  [local(): jnp.dot(stacked, operator[1], preferred_element_type=jnp.float32)]
    another operation x23 -> x12, other arithmetic: 6.93 us -> 5.05 us  [local(): current = jnp.stack([real_part, imag_part]).astype(jnp.bfloat16)]
  transfers between devices with their start and end apart: 10 -> 10, of which waited for: 3 -> 3; matrix products, arithmetic and copies ran while one was open for 3% -> 4% of each run, Pallas kernels for 0% -> 0%
where the time goes in v2:
time: 270 us; the launch traced here: 264 us
  waiting for transfers between devices  102 us (38%)
  matrix products  61.7 us (23%)
  Pallas kernels  46.8 us (17%)
  other arithmetic  15.8 us (6%)
  between operations  14.7 us (5%)
  starting transfers between devices  13 us (5%)
  local copies, waits for them, and re-layouts  10.2 us (4%)
    all_gather x2, waiting for transfers between devices, local(): gathered = lax.all_gather(lax.all_gather(mine, 'chip'), 'core')  99.6 us
    pallas_call x1, Pallas kernels, assemble_pallas(): pl.pallas_call(assemble_kernel, grid=(parts,), in_specs=[pl.BlockSpec(mem...  46.8 us
    dot_general x12, matrix products, local(): jnp.dot(stacked, operator[1], preferred_element_type=jnp.float32)  32.2 us
    dot_general x12, matrix products, local(): jnp.dot(stacked, operator[0], preferred_element_type=jnp.float32)  29.5 us
    ppermute x8, starting transfers between devices, upper_blocks(): lax.ppermute(send, AXES, perm=[(c, (c - s) % parts) for c in range(parts)])  12.9 us
    unnamed x51, local copies, waits for them, and re-layouts  8.23 us
  transfers between devices with their start and end apart: 10, of which 3 were waited for; matrix products, arithmetic and copies ran while one was open for 4% of the time, Pallas kernels for 0%

profile of v2, /device:TPU:0, one launch (start us, length us, event | category | flops | bytes accessed | tf_op | source)
XLA Modules:
  0.0 264.2 jit_solution(1113704086918833928)
XLA Ops:
  8.6 5.5 %collective-permute-start = (bf16[2,128,128]{1,2,0:T(8,128)(2,1)}, bf16[2,128,128]{1,2,0:T(8,128)(2,1)}, u32[]{:S(2)}, u32[]{:S(2)}) collective-permute-start(bf16[2,128,128]{1,2,0:T(8,128)(2,1)} %copy.26), channel_id=1, source_target_pairs={{0,15},{1,0},{2,1},{3,2},{4,3},{5,4},{6,5},{7,6},{8,7},{9,8},{10,9... | collective-permute-start | bytes 196616 | tf_op jit(solution)/shard_map/ppermute | solution.py:33
  20.1 4.4 %collective-permute-start.5 = (bf16[2,128,128]{1,2,0:T(8,128)(2,1)S(1)}, bf16[2,128,128]{1,2,0:T(8,128)(2,1)S(1)}, u32[]{:S(2)}, u32[]{:S(2)}) collective-permute-start(bf16[2,128,128]{1,2,0:T(8,128)(2,1)S(1)} %copy.31), channel_id=1, source_target_pairs={{0,10},{1,11},{2,12},{3,13},{4,14},{5,15},{6,0},{7,1},{8,2},{9,3},... | collective-permute-start | bytes 196616 | tf_op jit(solution)/shard_map/ppermute | solution.py:33
  34.7 79.4 %all-gather.5.cloned.1.call-done = bf16[72,2,128,128]{3,2,1,0:T(8,128)(2,1)} async-done(((bf16[9,2,128,128]{3,2,1,0:T(8,128)(2,1)}), bf16[72,2,128,128]{3,2,1,0:T(8,128)(2,1)}) %all-gather.5.cloned.1.call-update) | async-done | bytes 4718608 | tf_op jit(solution)/shard_map/all_gather | solution.py:111
  115.4 20.3 %all-gather.7.cloned.1.call-done = bf16[16,9,2,128,128]{4,3,2,1,0:T(8,128)(2,1)} async-done(((bf16[8,9,2,128,128]{4,3,2,1,0:T(8,128)(2,1)}), bf16[16,9,2,128,128]{4,3,2,1,0:T(8,128)(2,1)}) %all-gather.7.cloned.1.call-update) | async-done | bytes 9437200 | tf_op jit(solution)/shard_map/all_gather | solution.py:111
  135.6 46.8 %shard_map.46 = (bf16[2048,2048]{1,0:T(8,128)(2,1)}, bf16[2048,2048]{1,0:T(8,128)(2,1)}) custom-call(bf16[2,8,9,2,128,128]{5,4,3,2,1,0:T(8,128)(2,1)} %bitcast.208), custom_call_target="tpu_custom_call" | custom-call | tf_op jit(solution)/shard_map/pallas_call | solution.py:93
  182.4 5.9 %convolution_bitcast_fusion = f32[256,2048]{1,0:T(8,128)S(1)} fusion(bf16[256,2048]{1,0:T(8,128)(2,1)S(1)} %bitcast.206, bf16[2048,2048]{1,0:T(8,128)(2,1)} %get-tuple-element.8), kind=kOutput, calls=%fused_computation | convolution fusion | flops 2147483648 | bytes 11534336 | tf_op jit(solution)/shard_map/dot_general | solution.py:122
  188.3 2.4 convolution_bitcast_fusion.1
  192.1 2.4 fusion.70
  195.5 2.4 fusion.71
  198.4 2.4 fusion.72
  200.9 2.4 fusion.73
  203.8 2.6 fusion.74
  206.4 2.4 fusion.75
  209.3 2.4 fusion.76
  211.7 2.4 fusion.77
  214.7 2.4 fusion.78
  217.1 2.4 fusion.79
  220.0 2.6 fusion.80
  222.6 2.4 fusion.81
  228.0 2.4 fusion.83
  233.3 2.4 fusion.85
  236.2 2.7 %fusion.86 = f32[256,2048]{1,0:T(8,128)S(1)} fusion(bf16[256,2048]{1,0:T(8,128)(2,1)S(1)} %bitcast.228, bf16[2048,2048]{1,0:T(8,128)(2,1)S(1)} %copy-done.18), kind=kOutput, calls=%fused_computation.163 | convolution fusion | flops 2147483648 | bytes 11534336 | tf_op jit(solution)/shard_map/dot_general | solution.py:121
  238.9 2.4 fusion.87
  244.2 2.4 fusion.89
  (115 shorter events, 43.5 us)
Async XLA Ops:
  6.5 175.9 %copy-start = (bf16[2,128,2048]{2,1,0:T(8,128)(2,1)S(1)}, bf16[2,128,2048]{2,1,0:T(8,128)(2,1)}, u32[]{:S(2)}) copy-start(bf16[2,128,2048]{2,1,0:T(8,128)(2,1)} %param.5) | copy-start | bytes 3145732
  6.5 18.0 %copy-start.6 = (bf16[2,128,2048]{2,1,0:T(8,128)(2,1)S(1)}, bf16[2,128,2048]{2,1,0:T(8,128)(2,1)}, u32[]{:S(2)}) copy-start(bf16[2,128,2048]{2,1,0:T(8,128)(2,1)} %param.4) | copy-start | bytes 3145732
  6.5 12.2 %copy-start.17 = (f32[2048]{0:T(1024)S(1)}, f32[2048]{0:T(1024)}, u32[]{:S(2)}) copy-start(f32[2048]{0:T(1024)} %param.6) | copy-start | bytes 24580
  6.5 107.5 %all-gather.5.cloned.1.call-start = ((), (), s32[]{:S(2)}) async-start(), calls=%async_computation | async-start | bytes 5308416 | tf_op jit(solution)/shard_map/all_gather | solution.py:111
  8.6 11.5 %collective-permute-start = (bf16[2,128,128]{1,2,0:T(8,128)(2,1)}, bf16[2,128,128]{1,2,0:T(8,128)(2,1)}, u32[]{:S(2)}, u32[]{:S(2)}) collective-permute-start(bf16[2,128,128]{1,2,0:T(8,128)(2,1)} %copy.26), channel_id=1, source_target_pairs={{0,15},{1,0},{2,1},{3,2},{4,3},{5,4},{6,5},{7,6},{8,7},{9,8},{10,9... | collective-permute-start | bytes 196616 | tf_op jit(solution)/shard_map/ppermute | solution.py:33
  14.8 10.7 %collective-permute-start.1 = (bf16[2,128,128]{1,2,0:T(8,128)(2,1)}, bf16[2,128,128]{1,2,0:T(8,128)(2,1)}, u32[]{:S(2)}, u32[]{:S(2)}) collective-permute-start(bf16[2,128,128]{1,2,0:T(8,128)(2,1)} %copy.27), channel_id=1, source_target_pairs={{0,14},{1,15},{2,0},{3,1},{4,2},{5,3},{6,4},{7,5},{8,6},{9,7},{10,... | collective-permute-start | bytes 196616 | tf_op jit(solution)/shard_map/ppermute | solution.py:33
  16.1 10.4 %collective-permute-start.2 = (bf16[2,128,128]{1,2,0:T(8,128)(2,1)}, bf16[2,128,128]{1,2,0:T(8,128)(2,1)}, u32[]{:S(2)}, u32[]{:S(2)}) collective-permute-start(bf16[2,128,128]{1,2,0:T(8,128)(2,1)} %copy.28), channel_id=1, source_target_pairs={{0,13},{1,14},{2,15},{3,0},{4,1},{5,2},{6,3},{7,4},{8,5},{9,6},{10... | collective-permute-start | bytes 196616 | tf_op jit(solution)/shard_map/ppermute | solution.py:33
  17.2 12.0 %collective-permute-start.3 = (bf16[2,128,128]{1,2,0:T(8,128)(2,1)}, bf16[2,128,128]{1,2,0:T(8,128)(2,1)}, u32[]{:S(2)}, u32[]{:S(2)}) collective-permute-start(bf16[2,128,128]{1,2,0:T(8,128)(2,1)} %copy.29), channel_id=1, source_target_pairs={{0,12},{1,13},{2,14},{3,15},{4,0},{5,1},{6,2},{7,3},{8,4},{9,5},{1... | collective-permute-start | bytes 196616 | tf_op jit(solution)/shard_map/ppermute | solution.py:33
  18.3 11.8 %collective-permute-start.4 = (bf16[2,128,128]{1,2,0:T(8,128)(2,1)}, bf16[2,128,128]{1,2,0:T(8,128)(2,1)}, u32[]{:S(2)}, u32[]{:S(2)}) collective-permute-start(bf16[2,128,128]{1,2,0:T(8,128)(2,1)} %copy.30), channel_id=1, source_target_pairs={{0,11},{1,12},{2,13},{3,14},{4,15},{5,0},{6,1},{7,2},{8,3},{9,4},{... | collective-permute-start | bytes 196616 | tf_op jit(solution)/shard_map/ppermute | solution.py:33
  20.1 11.0 %collective-permute-start.5 = (bf16[2,128,128]{1,2,0:T(8,128)(2,1)S(1)}, bf16[2,128,128]{1,2,0:T(8,128)(2,1)S(1)}, u32[]{:S(2)}, u32[]{:S(2)}) collective-permute-start(bf16[2,128,128]{1,2,0:T(8,128)(2,1)S(1)} %copy.31), channel_id=1, source_target_pairs={{0,10},{1,11},{2,12},{3,13},{4,14},{5,15},{6,0},{7,1},{8,2},{9,3},... | collective-permute-start | bytes 196616 | tf_op jit(solution)/shard_map/ppermute | solution.py:33
  25.5 5.7 %collective-permute-start.6 = (bf16[2,128,128]{1,2,0:T(8,128)(2,1)S(1)}, bf16[2,128,128]{1,2,0:T(8,128)(2,1)S(1)}, u32[]{:S(2)}, u32[]{:S(2)}) collective-permute-start(bf16[2,128,128]{1,2,0:T(8,128)(2,1)S(1)} %copy.32), channel_id=1, source_target_pairs={{0,9},{1,10},{2,11},{3,12},{4,13},{5,14},{6,15},{7,0},{8,1},{9,2},... | collective-permute-start | bytes 196616 | tf_op jit(solution)/shard_map/ppermute | solution.py:33
  26.6 7.1 %collective-permute-start.7 = (bf16[2,128,128]{1,2,0:T(8,128)(2,1)S(1)}, bf16[2,128,128]{1,2,0:T(8,128)(2,1)S(1)}, u32[]{:S(2)}, u32[]{:S(2)}) collective-permute-start(bf16[2,128,128]{1,2,0:T(8,128)(2,1)S(1)} %copy.33), channel_id=1, source_target_pairs={{0,8},{1,9},{2,10},{3,11},{4,12},{5,13},{6,14},{7,15},{8,0},{9,1},... | collective-permute-start | bytes 196616 | tf_op jit(solution)/shard_map/ppermute | solution.py:33
  33.8 0.8 copy-start.8
  34.6 101.0 %all-gather.7.cloned.1.call-start = ((), (), s32[]{:S(2)}) async-start(), calls=%async_computation.1 | async-start | bytes 14155776 | tf_op jit(solution)/shard_map/all_gather | solution.py:111
  182.4 5.9 %copy-start.18 = (bf16[2048,2048]{1,0:T(8,128)(2,1)S(1)}, bf16[2048,2048]{1,0:T(8,128)(2,1)}, u32[]{:S(2)}) copy-start(bf16[2048,2048]{1,0:T(8,128)(2,1)} %get-tuple-element.7) | copy-start | bytes 25165828
  191.2 1.0 copy-start.4
  192.0 2.6 slice-start
  192.1 3.3 %slice-start.1 = ((s8[8388608]{0:T(1024)(128)(4,1)}), s8[4194304]{0:T(1024)(128)(4,1)S(1)}, s32[]{:S(2)}) async-start(s8[8388608]{0:T(1024)(128)(4,1)} %bitcast.234), calls=%async_computation.3 | async-start | bytes 8388608
  252.0 1.0 copy-start.3
  252.0 1.2 copy-start.5
  253.2 1.9 copy-start.7
  253.2 1.9 copy-start.9
  253.2 1.9 copy-start.10
  255.4 1.5 copy-start.1
  (7 other events, 5.4 us)
Sparse Core Ops, SparseCore 0:
  34.8 79.2 all-gather.4
  115.6 19.9 all-gather.6

commit v3 on v2

--- a/solution.py
+++ b/solution.py
@@ -61,21 +61,35 @@
     cores, chips, slots, _, rows, _ = g_ref.shape
     parts = chips * cores
     r = pl.program_id(0)
-    copies = []
-    for c in range(parts):
-        s = (c - r + parts) % parts
-        up = s <= parts // 2
-        a = jnp.where(up, r, c)
-        src = g_ref.at[a % cores, a // cores, jnp.where(up, s, parts - s)]
-        copy = pltpu.make_async_copy(src, buf.at[c], sem.at[c])
-        copy.start()
-        copies.append(copy)
-    for c in range(parts):
-        copies[c].wait()
+
+    def copies(row, slot):
+        out = []
+        for c in range(parts):
+            s = (c - row + parts) % parts
+            up = s <= parts // 2
+            a = jnp.where(up, row, c)
+            src = g_ref.at[a % cores, a // cores, jnp.where(up, s, parts - s)]
+            out.append(pltpu.make_async_copy(src, buf.at[slot, c], sem.at[slot, c]))
+        return out
+
+    @pl.when(r == 0)
+    def _():
+        for copy in copies(r, 0):
+            copy.start()
+
+    @pl.when(r + 1 < parts)
+    def _():
+        for copy in copies(r + 1, (r + 1) % 2):
+            copy.start()
+
+    slot = r % 2
+    eye = (lax.broadcasted_iota(jnp.int32, (rows, rows), 0) == lax.broadcasted_iota(jnp.int32, (rows, rows), 1)).astype(jnp.bfloat16)
+    for c, copy in enumerate(copies(r, slot)):
+        copy.wait()
         s = (c - r + parts) % parts
         up = s <= parts // 2
         for k, out in ((0, re_ref), (1, im_ref)):
-            block = buf[c, k]
+            block = buf[slot, c, k]
 
             @pl.when(up)
             def _():
@@ -83,7 +97,8 @@
 
             @pl.when(jnp.logical_not(up))
             def _():
-                out[:, c * rows:(c + 1) * rows] = block.astype(jnp.float32).T.astype(jnp.bfloat16)
+                flipped = lax.dot_general(eye, block, (((1,), (1,)), ((), ())), preferred_element_type=jnp.float32)
+                out[:, c * rows:(c + 1) * rows] = flipped.astype(jnp.bfloat16)
 
 
 def assemble_pallas(gathered, chips, cores):
@@ -96,7 +111,8 @@
         in_specs=[pl.BlockSpec(memory_space=pl.ANY)],
         out_specs=[pl.BlockSpec((rows, order), lambda r: (r, 0))] * 2,
         out_shape=[jax.ShapeDtypeStruct((order, order), jnp.bfloat16)] * 2,
-        scratch_shapes=[pltpu.VMEM((parts, 2, rows, rows), jnp.bfloat16), pltpu.SemaphoreType.DMA((parts,))],
+        scratch_shapes=[pltpu.VMEM((2, parts, 2, rows, rows), jnp.bfloat16), pltpu.SemaphoreType.DMA((2, parts))],
+        compiler_params=pltpu.CompilerParams(dimension_semantics=("arbitrary",)),
     )(gathered)
 
 
@@ -108,11 +124,11 @@
     parts = chips * cores
     here = lax.axis_index("chip") * cores + lax.axis_index("core")
     mine = upper_blocks(data_field, station_weight, parts, here)
-    gathered = lax.all_gather(lax.all_gather(mine, "chip"), "core")
+    gathered = lax.all_gather(mine, AXES)[None]
     if rows % 128 == 0:
-        operator = assemble_pallas(gathered, chips, cores)
+        operator = assemble_pallas(gathered, parts, 1)
     else:
-        operator = assemble(gathered, chips, cores)
+        operator = assemble(gathered, parts, 1)
     factor = 0.8 / math.sqrt(order)
     current = primary_field
     prediction = jnp.zeros(data_field.shape, jnp.float32)

time: 270 us -> 246 us (0.911)
  waiting for transfers between devices: 102 us -> 82 us
    all_gather x2 -> x1, waiting for transfers between devices: 99.6 us -> 79.6 us  [local(): gathered = lax.all_gather(mine, AXES)[None]]
    unnamed x51 -> x49, local copies, waits for them, and re-layouts: 8.23 us -> 7.59 us
  transfers between devices with their start and end apart: 10 -> 9, of which waited for: 3 -> 2; matrix products, arithmetic and copies ran while one was open for 4% -> 5% of each run, Pallas kernels for 0% -> 0%
where the time goes in v3:
time: 246 us; the launch traced here: 242 us
  waiting for transfers between devices  82 us (33%)
  matrix products  61.7 us (25%)
  Pallas kernels  44.7 us (18%)
  other arithmetic  15.8 us (6%)
  between operations  14.7 us (6%)
  starting transfers between devices  12.9 us (5%)
  local copies, waits for them, and re-layouts  10.4 us (4%)
    all_gather x1, waiting for transfers between devices, local(): gathered = lax.all_gather(mine, AXES)[None]  79.6 us
    pallas_call x1, Pallas kernels, assemble_pallas(): pl.pallas_call(assemble_kernel, grid=(parts,), in_specs=[pl.BlockSpec(mem...  44.7 us
    dot_general x12, matrix products, local(): jnp.dot(stacked, operator[1], preferred_element_type=jnp.float32)  32.2 us
    dot_general x12, matrix products, local(): jnp.dot(stacked, operator[0], preferred_element_type=jnp.float32)  29.4 us
    ppermute x8, starting transfers between devices, upper_blocks(): lax.ppermute(send, AXES, perm=[(c, (c - s) % parts) for c in range(parts)])  12.9 us
    unnamed x49, local copies, waits for them, and re-layouts  7.59 us
    unnamed x9, other arithmetic  5.1 us
    another operation x12, other arithmetic, local(): current = jnp.stack([real_part, imag_part]).astype(jnp.bfloat16)  5.05 us
  transfers between devices with their start and end apart: 9, of which 2 were waited for; matrix products, arithmetic and copies ran while one was open for 5% of the time, Pallas kernels for 0%

profile of v3, /device:TPU:0, one launch (start us, length us, event | category | flops | bytes accessed | tf_op | source)
XLA Modules:
  0.0 242.2 jit_solution(14345739376898146080)
XLA Ops:
  8.7 5.5 %collective-permute-start = (bf16[2,128,128]{1,2,0:T(8,128)(2,1)}, bf16[2,128,128]{1,2,0:T(8,128)(2,1)}, u32[]{:S(2)}, u32[]{:S(2)}) collective-permute-start(bf16[2,128,128]{1,2,0:T(8,128)(2,1)} %copy.26), channel_id=1, source_target_pairs={{0,15},{1,0},{2,1},{3,2},{4,3},{5,4},{6,5},{7,6},{8,7},{9,8},{10,9... | collective-permute-start | bytes 196616 | tf_op jit(solution)/shard_map/ppermute | solution.py:33
  20.2 4.4 %collective-permute-start.5 = (bf16[2,128,128]{1,2,0:T(8,128)(2,1)S(1)}, bf16[2,128,128]{1,2,0:T(8,128)(2,1)S(1)}, u32[]{:S(2)}, u32[]{:S(2)}) collective-permute-start(bf16[2,128,128]{1,2,0:T(8,128)(2,1)S(1)} %copy.31), channel_id=1, source_target_pairs={{0,10},{1,11},{2,12},{3,13},{4,14},{5,15},{6,0},{7,1},{8,2},{9,3},... | collective-permute-start | bytes 196616 | tf_op jit(solution)/shard_map/ppermute | solution.py:33
  36.1 79.6 %all-gather.3.cloned.1.call-done = bf16[144,2,128,128]{3,2,1,0:T(8,128)(2,1)} async-done(((bf16[9,2,128,128]{3,2,1,0:T(8,128)(2,1)}), bf16[144,2,128,128]{3,2,1,0:T(8,128)(2,1)}) %all-gather.3.cloned.1.call-update) | async-done | bytes 9437200 | tf_op jit(solution)/shard_map/all_gather | solution.py:127
  115.7 44.7 %shard_map.46 = (bf16[2048,2048]{1,0:T(8,128)(2,1)}, bf16[2048,2048]{1,0:T(8,128)(2,1)}) custom-call(bf16[1,16,9,2,128,128]{5,4,3,2,1,0:T(8,128)(2,1)} %bitcast.207), custom_call_target="tpu_custom_call" | custom-call | tf_op jit(solution)/shard_map/pallas_call | solution.py:108
  160.4 5.9 %convolution_bitcast_fusion = f32[256,2048]{1,0:T(8,128)S(1)} fusion(bf16[256,2048]{1,0:T(8,128)(2,1)S(1)} %bitcast.205, bf16[2048,2048]{1,0:T(8,128)(2,1)} %get-tuple-element.8), kind=kOutput, calls=%fused_computation | convolution fusion | flops 2147483648 | bytes 11534336 | tf_op jit(solution)/shard_map/dot_general | solution.py:138
  166.2 2.4 convolution_bitcast_fusion.1
  170.1 2.4 fusion.70
  173.4 2.4 fusion.71
  176.4 2.4 fusion.72
  178.8 2.4 fusion.73
  181.8 2.6 %fusion.74 = f32[256,2048]{1,0:T(8,128)S(1)} fusion(bf16[256,2048]{1,0:T(8,128)(2,1)S(1)} %bitcast.214, bf16[2048,2048]{1,0:T(8,128)(2,1)S(1)} %copy-done.17), kind=kOutput, calls=%fused_computation.151 | convolution fusion | flops 2147483648 | bytes 11534336 | tf_op jit(solution)/shard_map/dot_general | solution.py:137
  184.3 2.4 fusion.75
  189.7 2.4 fusion.77
  195.0 2.4 fusion.79
  198.0 2.6 %fusion.80 = f32[256,2048]{1,0:T(8,128)S(1)} fusion(bf16[256,2048]{1,0:T(8,128)(2,1)S(1)} %bitcast.220, bf16[2048,2048]{1,0:T(8,128)(2,1)S(1)} %copy-done.17), kind=kOutput, calls=%fused_computation.157 | convolution fusion | flops 2147483648 | bytes 11534336 | tf_op jit(solution)/shard_map/dot_general | solution.py:137
  200.6 2.4 fusion.81
  205.9 2.4 fusion.83
  211.2 2.4 fusion.85
  214.2 2.6 %fusion.86 = f32[256,2048]{1,0:T(8,128)S(1)} fusion(bf16[256,2048]{1,0:T(8,128)(2,1)S(1)} %bitcast.226, bf16[2048,2048]{1,0:T(8,128)(2,1)S(1)} %copy-done.17), kind=kOutput, calls=%fused_computation.163 | convolution fusion | flops 2147483648 | bytes 11534336 | tf_op jit(solution)/shard_map/dot_general | solution.py:137
  216.8 2.4 fusion.87
  219.8 2.4 fusion.88
  222.2 2.4 fusion.89
  225.1 2.4 fusion.90
  227.5 2.4 fusion.91
  (110 shorter events, 41.2 us)
Async XLA Ops:
  6.5 153.8 %copy-start = (bf16[2,128,2048]{2,1,0:T(8,128)(2,1)S(1)}, bf16[2,128,2048]{2,1,0:T(8,128)(2,1)}, u32[]{:S(2)}) copy-start(bf16[2,128,2048]{2,1,0:T(8,128)(2,1)} %param.5) | copy-start | bytes 3145732
  6.5 18.1 %copy-start.6 = (bf16[2,128,2048]{2,1,0:T(8,128)(2,1)S(1)}, bf16[2,128,2048]{2,1,0:T(8,128)(2,1)}, u32[]{:S(2)}) copy-start(bf16[2,128,2048]{2,1,0:T(8,128)(2,1)} %param.4) | copy-start | bytes 3145732
  6.5 12.2 %copy-start.16 = (f32[2048]{0:T(1024)S(1)}, f32[2048]{0:T(1024)}, u32[]{:S(2)}) copy-start(f32[2048]{0:T(1024)} %param.6) | copy-start | bytes 24580
  6.5 109.1 %all-gather.3.cloned.1.call-start = ((), (), s32[]{:S(2)}) async-start(), calls=%async_computation | async-start | bytes 10027008 | tf_op jit(solution)/shard_map/all_gather | solution.py:127
  8.7 11.5 %collective-permute-start = (bf16[2,128,128]{1,2,0:T(8,128)(2,1)}, bf16[2,128,128]{1,2,0:T(8,128)(2,1)}, u32[]{:S(2)}, u32[]{:S(2)}) collective-permute-start(bf16[2,128,128]{1,2,0:T(8,128)(2,1)} %copy.26), channel_id=1, source_target_pairs={{0,15},{1,0},{2,1},{3,2},{4,3},{5,4},{6,5},{7,6},{8,7},{9,8},{10,9... | collective-permute-start | bytes 196616 | tf_op jit(solution)/shard_map/ppermute | solution.py:33
  14.9 10.7 %collective-permute-start.1 = (bf16[2,128,128]{1,2,0:T(8,128)(2,1)}, bf16[2,128,128]{1,2,0:T(8,128)(2,1)}, u32[]{:S(2)}, u32[]{:S(2)}) collective-permute-start(bf16[2,128,128]{1,2,0:T(8,128)(2,1)} %copy.27), channel_id=1, source_target_pairs={{0,14},{1,15},{2,0},{3,1},{4,2},{5,3},{6,4},{7,5},{8,6},{9,7},{10,... | collective-permute-start | bytes 196616 | tf_op jit(solution)/shard_map/ppermute | solution.py:33
  16.2 10.5 %collective-permute-start.2 = (bf16[2,128,128]{1,2,0:T(8,128)(2,1)}, bf16[2,128,128]{1,2,0:T(8,128)(2,1)}, u32[]{:S(2)}, u32[]{:S(2)}) collective-permute-start(bf16[2,128,128]{1,2,0:T(8,128)(2,1)} %copy.28), channel_id=1, source_target_pairs={{0,13},{1,14},{2,15},{3,0},{4,1},{5,2},{6,3},{7,4},{8,5},{9,6},{10... | collective-permute-start | bytes 196616 | tf_op jit(solution)/shard_map/ppermute | solution.py:33
  17.2 12.0 %collective-permute-start.3 = (bf16[2,128,128]{1,2,0:T(8,128)(2,1)}, bf16[2,128,128]{1,2,0:T(8,128)(2,1)}, u32[]{:S(2)}, u32[]{:S(2)}) collective-permute-start(bf16[2,128,128]{1,2,0:T(8,128)(2,1)} %copy.29), channel_id=1, source_target_pairs={{0,12},{1,13},{2,14},{3,15},{4,0},{5,1},{6,2},{7,3},{8,4},{9,5},{1... | collective-permute-start | bytes 196616 | tf_op jit(solution)/shard_map/ppermute | solution.py:33
  18.4 11.8 %collective-permute-start.4 = (bf16[2,128,128]{1,2,0:T(8,128)(2,1)}, bf16[2,128,128]{1,2,0:T(8,128)(2,1)}, u32[]{:S(2)}, u32[]{:S(2)}) collective-permute-start(bf16[2,128,128]{1,2,0:T(8,128)(2,1)} %copy.30), channel_id=1, source_target_pairs={{0,11},{1,12},{2,13},{3,14},{4,15},{5,0},{6,1},{7,2},{8,3},{9,4},{... | collective-permute-start | bytes 196616 | tf_op jit(solution)/shard_map/ppermute | solution.py:33
  20.2 11.0 %collective-permute-start.5 = (bf16[2,128,128]{1,2,0:T(8,128)(2,1)S(1)}, bf16[2,128,128]{1,2,0:T(8,128)(2,1)S(1)}, u32[]{:S(2)}, u32[]{:S(2)}) collective-permute-start(bf16[2,128,128]{1,2,0:T(8,128)(2,1)S(1)} %copy.31), channel_id=1, source_target_pairs={{0,10},{1,11},{2,12},{3,13},{4,14},{5,15},{6,0},{7,1},{8,2},{9,3},... | collective-permute-start | bytes 196616 | tf_op jit(solution)/shard_map/ppermute | solution.py:33
  25.6 5.7 %collective-permute-start.6 = (bf16[2,128,128]{1,2,0:T(8,128)(2,1)S(1)}, bf16[2,128,128]{1,2,0:T(8,128)(2,1)S(1)}, u32[]{:S(2)}, u32[]{:S(2)}) collective-permute-start(bf16[2,128,128]{1,2,0:T(8,128)(2,1)S(1)} %copy.32), channel_id=1, source_target_pairs={{0,9},{1,10},{2,11},{3,12},{4,13},{5,14},{6,15},{7,0},{8,1},{9,2},... | collective-permute-start | bytes 196616 | tf_op jit(solution)/shard_map/ppermute | solution.py:33
  26.6 7.1 %collective-permute-start.7 = (bf16[2,128,128]{1,2,0:T(8,128)(2,1)S(1)}, bf16[2,128,128]{1,2,0:T(8,128)(2,1)S(1)}, u32[]{:S(2)}, u32[]{:S(2)}) collective-permute-start(bf16[2,128,128]{1,2,0:T(8,128)(2,1)S(1)} %copy.33), channel_id=1, source_target_pairs={{0,8},{1,9},{2,10},{3,11},{4,12},{5,13},{6,14},{7,15},{8,0},{9,1},... | collective-permute-start | bytes 196616 | tf_op jit(solution)/shard_map/ppermute | solution.py:33
  33.8 0.8 copy-start.8
  160.4 5.9 %copy-start.17 = (bf16[2048,2048]{1,0:T(8,128)(2,1)S(1)}, bf16[2048,2048]{1,0:T(8,128)(2,1)}, u32[]{:S(2)}) copy-start(bf16[2048,2048]{1,0:T(8,128)(2,1)} %get-tuple-element.7) | copy-start | bytes 25165828
  169.1 0.8 copy-start.2
  169.1 1.0 copy-start.4
  169.9 2.6 %slice-start = ((s8[8388608]{0:T(1024)(128)(4,1)}), s8[4194304]{0:T(1024)(128)(4,1)S(1)}, s32[]{:S(2)}) async-start(s8[8388608]{0:T(1024)(128)(4,1)} %bitcast.232), calls=%async_computation.1 | async-start | bytes 8388608
  170.1 3.3 %slice-start.1 = ((s8[8388608]{0:T(1024)(128)(4,1)}), s8[4194304]{0:T(1024)(128)(4,1)S(1)}, s32[]{:S(2)}) async-start(s8[8388608]{0:T(1024)(128)(4,1)} %bitcast.232), calls=%async_computation.2 | async-start | bytes 8388608
  229.9 1.0 copy-start.3
  229.9 1.2 copy-start.5
  231.1 1.9 copy-start.7
  231.1 1.9 copy-start.9
  231.1 1.9 copy-start.10
  233.4 1.5 copy-start.1
  (5 other events, 3.9 us)
Sparse Core Ops, SparseCore 0:
  34.8 80.8 all-gather.2

commit v4 on v3

--- a/solution.py
+++ b/solution.py
@@ -57,19 +57,16 @@
     return blocks.transpose(2, 0, 3, 1, 4).reshape(2, parts * rows, parts * rows)
 
 
-def assemble_kernel(g_ref, re_ref, im_ref, buf, sem):
+def assemble_kernel(g_ref, re_ref, im_ref, upper, lower, sem):
     cores, chips, slots, _, rows, _ = g_ref.shape
     parts = chips * cores
     r = pl.program_id(0)
 
     def copies(row, slot):
-        out = []
-        for c in range(parts):
-            s = (c - row + parts) % parts
-            up = s <= parts // 2
-            a = jnp.where(up, row, c)
-            src = g_ref.at[a % cores, a // cores, jnp.where(up, s, parts - s)]
-            out.append(pltpu.make_async_copy(src, buf.at[slot, c], sem.at[slot, c]))
+        out = [pltpu.make_async_copy(g_ref.at[row % cores, row // cores], upper.at[slot], sem.at[slot, 0])]
+        for t in range(1, parts // 2):
+            a = (row + parts - t) % parts
+            out.append(pltpu.make_async_copy(g_ref.at[a % cores, a // cores, t], lower.at[slot, t], sem.at[slot, t]))
         return out
 
     @pl.when(r == 0)
@@ -83,22 +80,16 @@
             copy.start()
 
     slot = r % 2
-    eye = (lax.broadcasted_iota(jnp.int32, (rows, rows), 0) == lax.broadcasted_iota(jnp.int32, (rows, rows), 1)).astype(jnp.bfloat16)
-    for c, copy in enumerate(copies(r, slot)):
+    for copy in copies(r, slot):
         copy.wait()
-        s = (c - r + parts) % parts
-        up = s <= parts // 2
+    for s in range(parts):
+        col = pl.multiple_of(((r + s) % parts) * rows, rows)
         for k, out in ((0, re_ref), (1, im_ref)):
-            block = buf[slot, c, k]
-
-            @pl.when(up)
-            def _():
-                out[:, c * rows:(c + 1) * rows] = block
-
-            @pl.when(jnp.logical_not(up))
-            def _():
-                flipped = lax.dot_general(eye, block, (((1,), (1,)), ((), ())), preferred_element_type=jnp.float32)
-                out[:, c * rows:(c + 1) * rows] = flipped.astype(jnp.bfloat16)
+            if s <= parts // 2:
+                block = upper[slot, s, k]
+            else:
+                block = lower[slot, parts - s, k].astype(jnp.float32).T.astype(jnp.bfloat16)
+            out[:, pl.ds(col, rows)] = block
 
 
 def assemble_pallas(gathered, chips, cores):
@@ -111,7 +102,11 @@
         in_specs=[pl.BlockSpec(memory_space=pl.ANY)],
         out_specs=[pl.BlockSpec((rows, order), lambda r: (r, 0))] * 2,
         out_shape=[jax.ShapeDtypeStruct((order, order), jnp.bfloat16)] * 2,
-        scratch_shapes=[pltpu.VMEM((2, parts, 2, rows, rows), jnp.bfloat16), pltpu.SemaphoreType.DMA((2, parts))],
+        scratch_shapes=[
+            pltpu.VMEM((2, gathered.shape[2], 2, rows, rows), jnp.bfloat16),
+            pltpu.VMEM((2, parts // 2, 2, rows, rows), jnp.bfloat16),
+            pltpu.SemaphoreType.DMA((2, parts // 2)),
+        ],
         compiler_params=pltpu.CompilerParams(dimension_semantics=("arbitrary",)),
     )(gathered)
 

time: 246 us -> 220 us (0.89)
  Pallas kernels: 44.7 us -> 19.1 us
    pallas_call x1, Pallas kernels: 44.7 us -> 19.1 us  [assemble_pallas(): pl.pallas_call(assemble_kernel, grid=(parts,), in_specs=[pl.BlockSpec(mem...]
where the time goes in v4:
time: 220 us; the launch traced here: 217 us
  waiting for transfers between devices  82 us (37%)
  matrix products  61.7 us (28%)
  Pallas kernels  19.1 us (9%)
  other arithmetic  15.8 us (7%)
  between operations  14.7 us (7%)
  starting transfers between devices  12.9 us (6%)
  local copies, waits for them, and re-layouts  10.4 us (5%)
    all_gather x1, waiting for transfers between devices, local(): gathered = lax.all_gather(mine, AXES)[None]  79.6 us
    dot_general x12, matrix products, local(): jnp.dot(stacked, operator[1], preferred_element_type=jnp.float32)  32.2 us
    dot_general x12, matrix products, local(): jnp.dot(stacked, operator[0], preferred_element_type=jnp.float32)  29.5 us
    pallas_call x1, Pallas kernels, assemble_pallas(): pl.pallas_call(assemble_kernel, grid=(parts,), in_specs=[pl.BlockSpec(mem...  19.1 us
    ppermute x8, starting transfers between devices, upper_blocks(): lax.ppermute(send, AXES, perm=[(c, (c - s) % parts) for c in range(parts)])  12.9 us
    unnamed x49, local copies, waits for them, and re-layouts  7.59 us
    unnamed x9, other arithmetic  5.1 us
    another operation x12, other arithmetic, local(): current = jnp.stack([real_part, imag_part]).astype(jnp.bfloat16)  5.05 us
  transfers between devices with their start and end apart: 9, of which 2 were waited for; matrix products, arithmetic and copies ran while one was open for 5% of the time, Pallas kernels for 0%

profile of v4, /device:TPU:0, one launch (start us, length us, event | category | flops | bytes accessed | tf_op | source)
XLA Modules:
  0.0 216.6 jit_solution(13560629905317151620)
XLA Ops:
  8.7 5.5 %collective-permute-start = (bf16[2,128,128]{1,2,0:T(8,128)(2,1)}, bf16[2,128,128]{1,2,0:T(8,128)(2,1)}, u32[]{:S(2)}, u32[]{:S(2)}) collective-permute-start(bf16[2,128,128]{1,2,0:T(8,128)(2,1)} %copy.26), channel_id=1, source_target_pairs={{0,15},{1,0},{2,1},{3,2},{4,3},{5,4},{6,5},{7,6},{8,7},{9,8},{10,9... | collective-permute-start | bytes 196616 | tf_op jit(solution)/shard_map/ppermute | solution.py:33
  20.2 4.4 %collective-permute-start.5 = (bf16[2,128,128]{1,2,0:T(8,128)(2,1)S(1)}, bf16[2,128,128]{1,2,0:T(8,128)(2,1)S(1)}, u32[]{:S(2)}, u32[]{:S(2)}) collective-permute-start(bf16[2,128,128]{1,2,0:T(8,128)(2,1)S(1)} %copy.31), channel_id=1, source_target_pairs={{0,10},{1,11},{2,12},{3,13},{4,14},{5,15},{6,0},{7,1},{8,2},{9,3},... | collective-permute-start | bytes 196616 | tf_op jit(solution)/shard_map/ppermute | solution.py:33
  36.1 79.6 %all-gather.3.cloned.1.call-done = bf16[144,2,128,128]{3,2,1,0:T(8,128)(2,1)} async-done(((bf16[9,2,128,128]{3,2,1,0:T(8,128)(2,1)}), bf16[144,2,128,128]{3,2,1,0:T(8,128)(2,1)}) %all-gather.3.cloned.1.call-update) | async-done | bytes 9437200 | tf_op jit(solution)/shard_map/all_gather | solution.py:122
  115.7 19.1 %shard_map.46 = (bf16[2048,2048]{1,0:T(8,128)(2,1)}, bf16[2048,2048]{1,0:T(8,128)(2,1)}) custom-call(bf16[1,16,9,2,128,128]{5,4,3,2,1,0:T(8,128)(2,1)} %bitcast.207), custom_call_target="tpu_custom_call" | custom-call | tf_op jit(solution)/shard_map/pallas_call | solution.py:99
  134.8 5.9 %convolution_bitcast_fusion = f32[256,2048]{1,0:T(8,128)S(1)} fusion(bf16[256,2048]{1,0:T(8,128)(2,1)S(1)} %bitcast.205, bf16[2048,2048]{1,0:T(8,128)(2,1)} %get-tuple-element.8), kind=kOutput, calls=%fused_computation | convolution fusion | flops 2147483648 | bytes 11534336 | tf_op jit(solution)/shard_map/dot_general | solution.py:133
  140.7 2.4 %convolution_bitcast_fusion.1 = f32[256,2048]{1,0:T(8,128)S(1)} fusion(bf16[256,2048]{1,0:T(8,128)(2,1)S(1)} %bitcast.206, bf16[2048,2048]{1,0:T(8,128)(2,1)S(1)} %copy-done.17), kind=kOutput, calls=%fused_computation.1 | convolution fusion | flops 2147483648 | bytes 11534336 | tf_op jit(solution)/shard_map/dot_general | solution.py:132
  144.5 2.4 %fusion.70 = f32[256,2048]{1,0:T(8,128)S(1)} fusion(bf16[256,2048]{1,0:T(8,128)(2,1)S(1)} %bitcast.210, bf16[2048,2048]{1,0:T(8,128)(2,1)S(1)} %copy-done.17), kind=kOutput, calls=%fused_computation.147 | convolution fusion | flops 2147483648 | bytes 11534336 | tf_op jit(solution)/shard_map/dot_general | solution.py:132
  147.9 2.4 %fusion.71 = f32[256,2048]{1,0:T(8,128)S(1)} fusion(bf16[256,2048]{1,0:T(8,128)(2,1)S(1)} %bitcast.211, bf16[2048,2048]{1,0:T(8,128)(2,1)S(1)} %bitcast.233), kind=kOutput, calls=%fused_computation.148 | convolution fusion | flops 2147483648 | bytes 11534336 | tf_op jit(solution)/shard_map/dot_general | solution.py:133
  150.8 2.4 %fusion.72 = f32[256,2048]{1,0:T(8,128)S(1)} fusion(bf16[256,2048]{1,0:T(8,128)(2,1)S(1)} %bitcast.212, bf16[2048,2048]{1,0:T(8,128)(2,1)S(1)} %copy-done.17), kind=kOutput, calls=%fused_computation.149 | convolution fusion | flops 2147483648 | bytes 11534336 | tf_op jit(solution)/shard_map/dot_general | solution.py:132
  153.2 2.4 %fusion.73 = f32[256,2048]{1,0:T(8,128)S(1)} fusion(bf16[256,2048]{1,0:T(8,128)(2,1)S(1)} %bitcast.213, bf16[2048,2048]{1,0:T(8,128)(2,1)S(1)} %bitcast.233), kind=kOutput, calls=%fused_computation.150 | convolution fusion | flops 2147483648 | bytes 11534336 | tf_op jit(solution)/shard_map/dot_general | solution.py:133
  156.2 2.6 %fusion.74 = f32[256,2048]{1,0:T(8,128)S(1)} fusion(bf16[256,2048]{1,0:T(8,128)(2,1)S(1)} %bitcast.214, bf16[2048,2048]{1,0:T(8,128)(2,1)S(1)} %copy-done.17), kind=kOutput, calls=%fused_computation.151 | convolution fusion | flops 2147483648 | bytes 11534336 | tf_op jit(solution)/shard_map/dot_general | solution.py:132
  158.8 2.4 %fusion.75 = f32[256,2048]{1,0:T(8,128)S(1)} fusion(bf16[256,2048]{1,0:T(8,128)(2,1)S(1)} %bitcast.215, bf16[2048,2048]{1,0:T(8,128)(2,1)S(1)} %bitcast.233), kind=kOutput, calls=%fused_computation.152 | convolution fusion | flops 2147483648 | bytes 11534336 | tf_op jit(solution)/shard_map/dot_general | solution.py:133
  161.7 2.4 %fusion.76 = f32[256,2048]{1,0:T(8,128)S(1)} fusion(bf16[256,2048]{1,0:T(8,128)(2,1)S(1)} %bitcast.216, bf16[2048,2048]{1,0:T(8,128)(2,1)S(1)} %copy-done.17), kind=kOutput, calls=%fused_computation.153 | convolution fusion | flops 2147483648 | bytes 11534336 | tf_op jit(solution)/shard_map/dot_general | solution.py:132
  164.1 2.4 %fusion.77 = f32[256,2048]{1,0:T(8,128)S(1)} fusion(bf16[256,2048]{1,0:T(8,128)(2,1)S(1)} %bitcast.217, bf16[2048,2048]{1,0:T(8,128)(2,1)S(1)} %bitcast.233), kind=kOutput, calls=%fused_computation.154 | convolution fusion | flops 2147483648 | bytes 11534336 | tf_op jit(solution)/shard_map/dot_general | solution.py:133
  167.1 2.4 %fusion.78 = f32[256,2048]{1,0:T(8,128)S(1)} fusion(bf16[256,2048]{1,0:T(8,128)(2,1)S(1)} %bitcast.218, bf16[2048,2048]{1,0:T(8,128)(2,1)S(1)} %copy-done.17), kind=kOutput, calls=%fused_computation.155 | convolution fusion | flops 2147483648 | bytes 11534336 | tf_op jit(solution)/shard_map/dot_general | solution.py:132
  169.5 2.4 %fusion.79 = f32[256,2048]{1,0:T(8,128)S(1)} fusion(bf16[256,2048]{1,0:T(8,128)(2,1)S(1)} %bitcast.219, bf16[2048,2048]{1,0:T(8,128)(2,1)S(1)} %bitcast.233), kind=kOutput, calls=%fused_computation.156 | convolution fusion | flops 2147483648 | bytes 11534336 | tf_op jit(solution)/shard_map/dot_general | solution.py:133
  172.4 2.6 %fusion.80 = f32[256,2048]{1,0:T(8,128)S(1)} fusion(bf16[256,2048]{1,0:T(8,128)(2,1)S(1)} %bitcast.220, bf16[2048,2048]{1,0:T(8,128)(2,1)S(1)} %copy-done.17), kind=kOutput, calls=%fused_computation.157 | convolution fusion | flops 2147483648 | bytes 11534336 | tf_op jit(solution)/shard_map/dot_general | solution.py:132
  175.0 2.4 %fusion.81 = f32[256,2048]{1,0:T(8,128)S(1)} fusion(bf16[256,2048]{1,0:T(8,128)(2,1)S(1)} %bitcast.221, bf16[2048,2048]{1,0:T(8,128)(2,1)S(1)} %bitcast.233), kind=kOutput, calls=%fused_computation.158 | convolution fusion | flops 2147483648 | bytes 11534336 | tf_op jit(solution)/shard_map/dot_general | solution.py:133
  180.4 2.4 %fusion.83 = f32[256,2048]{1,0:T(8,128)S(1)} fusion(bf16[256,2048]{1,0:T(8,128)(2,1)S(1)} %bitcast.223, bf16[2048,2048]{1,0:T(8,128)(2,1)S(1)} %bitcast.233), kind=kOutput, calls=%fused_computation.160 | convolution fusion | flops 2147483648 | bytes 11534336 | tf_op jit(solution)/shard_map/dot_general | solution.py:133
  185.7 2.4 %fusion.85 = f32[256,2048]{1,0:T(8,128)S(1)} fusion(bf16[256,2048]{1,0:T(8,128)(2,1)S(1)} %bitcast.225, bf16[2048,2048]{1,0:T(8,128)(2,1)S(1)} %bitcast.233), kind=kOutput, calls=%fused_computation.162 | convolution fusion | flops 2147483648 | bytes 11534336 | tf_op jit(solution)/shard_map/dot_general | solution.py:133
  188.6 2.7 %fusion.86 = f32[256,2048]{1,0:T(8,128)S(1)} fusion(bf16[256,2048]{1,0:T(8,128)(2,1)S(1)} %bitcast.226, bf16[2048,2048]{1,0:T(8,128)(2,1)S(1)} %copy-done.17), kind=kOutput, calls=%fused_computation.163 | convolution fusion | flops 2147483648 | bytes 11534336 | tf_op jit(solution)/shard_map/dot_general | solution.py:132
  191.3 2.4 %fusion.87 = f32[256,2048]{1,0:T(8,128)S(1)} fusion(bf16[256,2048]{1,0:T(8,128)(2,1)S(1)} %bitcast.227, bf16[2048,2048]{1,0:T(8,128)(2,1)S(1)} %bitcast.233), kind=kOutput, calls=%fused_computation.164 | convolution fusion | flops 2147483648 | bytes 11534336 | tf_op jit(solution)/shard_map/dot_general | solution.py:133
  196.6 2.4 %fusion.89 = f32[256,2048]{1,0:T(8,128)S(1)} fusion(bf16[256,2048]{1,0:T(8,128)(2,1)S(1)} %bitcast.229, bf16[2048,2048]{1,0:T(8,128)(2,1)S(1)} %bitcast.233), kind=kOutput, calls=%fused_computation.166 | convolution fusion | flops 2147483648 | bytes 11534336 | tf_op jit(solution)/shard_map/dot_general | solution.py:133
  202.0 2.4 %fusion.91 = f32[256,2048]{1,0:T(8,128)S(1)} fusion(bf16[256,2048]{1,0:T(8,128)(2,1)S(1)} %bitcast.209, bf16[2048,2048]{1,0:T(8,128)(2,1)S(1)} %bitcast.233), kind=kOutput, calls=%fused_computation.168 | convolution fusion | flops 2147483648 | bytes 11534336 | tf_op jit(solution)/shard_map/dot_general | solution.py:133
  (110 shorter events, 41.2 us)
Async XLA Ops:
  6.5 128.3 %copy-start = (bf16[2,128,2048]{2,1,0:T(8,128)(2,1)S(1)}, bf16[2,128,2048]{2,1,0:T(8,128)(2,1)}, u32[]{:S(2)}) copy-start(bf16[2,128,2048]{2,1,0:T(8,128)(2,1)} %param.5) | copy-start | bytes 3145732
  6.5 18.1 %copy-start.6 = (bf16[2,128,2048]{2,1,0:T(8,128)(2,1)S(1)}, bf16[2,128,2048]{2,1,0:T(8,128)(2,1)}, u32[]{:S(2)}) copy-start(bf16[2,128,2048]{2,1,0:T(8,128)(2,1)} %param.4) | copy-start | bytes 3145732
  6.5 12.2 %copy-start.16 = (f32[2048]{0:T(1024)S(1)}, f32[2048]{0:T(1024)}, u32[]{:S(2)}) copy-start(f32[2048]{0:T(1024)} %param.6) | copy-start | bytes 24580
  6.5 109.1 %all-gather.3.cloned.1.call-start = ((), (), s32[]{:S(2)}) async-start(), calls=%async_computation | async-start | bytes 10027008 | tf_op jit(solution)/shard_map/all_gather | solution.py:122
  8.7 11.5 %collective-permute-start = (bf16[2,128,128]{1,2,0:T(8,128)(2,1)}, bf16[2,128,128]{1,2,0:T(8,128)(2,1)}, u32[]{:S(2)}, u32[]{:S(2)}) collective-permute-start(bf16[2,128,128]{1,2,0:T(8,128)(2,1)} %copy.26), channel_id=1, source_target_pairs={{0,15},{1,0},{2,1},{3,2},{4,3},{5,4},{6,5},{7,6},{8,7},{9,8},{10,9... | collective-permute-start | bytes 196616 | tf_op jit(solution)/shard_map/ppermute | solution.py:33
  14.9 10.7 %collective-permute-start.1 = (bf16[2,128,128]{1,2,0:T(8,128)(2,1)}, bf16[2,128,128]{1,2,0:T(8,128)(2,1)}, u32[]{:S(2)}, u32[]{:S(2)}) collective-permute-start(bf16[2,128,128]{1,2,0:T(8,128)(2,1)} %copy.27), channel_id=1, source_target_pairs={{0,14},{1,15},{2,0},{3,1},{4,2},{5,3},{6,4},{7,5},{8,6},{9,7},{10,... | collective-permute-start | bytes 196616 | tf_op jit(solution)/shard_map/ppermute | solution.py:33
  16.2 10.5 %collective-permute-start.2 = (bf16[2,128,128]{1,2,0:T(8,128)(2,1)}, bf16[2,128,128]{1,2,0:T(8,128)(2,1)}, u32[]{:S(2)}, u32[]{:S(2)}) collective-permute-start(bf16[2,128,128]{1,2,0:T(8,128)(2,1)} %copy.28), channel_id=1, source_target_pairs={{0,13},{1,14},{2,15},{3,0},{4,1},{5,2},{6,3},{7,4},{8,5},{9,6},{10... | collective-permute-start | bytes 196616 | tf_op jit(solution)/shard_map/ppermute | solution.py:33
  17.2 12.0 %collective-permute-start.3 = (bf16[2,128,128]{1,2,0:T(8,128)(2,1)}, bf16[2,128,128]{1,2,0:T(8,128)(2,1)}, u32[]{:S(2)}, u32[]{:S(2)}) collective-permute-start(bf16[2,128,128]{1,2,0:T(8,128)(2,1)} %copy.29), channel_id=1, source_target_pairs={{0,12},{1,13},{2,14},{3,15},{4,0},{5,1},{6,2},{7,3},{8,4},{9,5},{1... | collective-permute-start | bytes 196616 | tf_op jit(solution)/shard_map/ppermute | solution.py:33
  18.4 11.8 %collective-permute-start.4 = (bf16[2,128,128]{1,2,0:T(8,128)(2,1)}, bf16[2,128,128]{1,2,0:T(8,128)(2,1)}, u32[]{:S(2)}, u32[]{:S(2)}) collective-permute-start(bf16[2,128,128]{1,2,0:T(8,128)(2,1)} %copy.30), channel_id=1, source_target_pairs={{0,11},{1,12},{2,13},{3,14},{4,15},{5,0},{6,1},{7,2},{8,3},{9,4},{... | collective-permute-start | bytes 196616 | tf_op jit(solution)/shard_map/ppermute | solution.py:33
  20.2 11.0 %collective-permute-start.5 = (bf16[2,128,128]{1,2,0:T(8,128)(2,1)S(1)}, bf16[2,128,128]{1,2,0:T(8,128)(2,1)S(1)}, u32[]{:S(2)}, u32[]{:S(2)}) collective-permute-start(bf16[2,128,128]{1,2,0:T(8,128)(2,1)S(1)} %copy.31), channel_id=1, source_target_pairs={{0,10},{1,11},{2,12},{3,13},{4,14},{5,15},{6,0},{7,1},{8,2},{9,3},... | collective-permute-start | bytes 196616 | tf_op jit(solution)/shard_map/ppermute | solution.py:33
  25.6 5.7 %collective-permute-start.6 = (bf16[2,128,128]{1,2,0:T(8,128)(2,1)S(1)}, bf16[2,128,128]{1,2,0:T(8,128)(2,1)S(1)}, u32[]{:S(2)}, u32[]{:S(2)}) collective-permute-start(bf16[2,128,128]{1,2,0:T(8,128)(2,1)S(1)} %copy.32), channel_id=1, source_target_pairs={{0,9},{1,10},{2,11},{3,12},{4,13},{5,14},{6,15},{7,0},{8,1},{9,2},... | collective-permute-start | bytes 196616 | tf_op jit(solution)/shard_map/ppermute | solution.py:33
  26.6 7.1 %collective-permute-start.7 = (bf16[2,128,128]{1,2,0:T(8,128)(2,1)S(1)}, bf16[2,128,128]{1,2,0:T(8,128)(2,1)S(1)}, u32[]{:S(2)}, u32[]{:S(2)}) collective-permute-start(bf16[2,128,128]{1,2,0:T(8,128)(2,1)S(1)} %copy.33), channel_id=1, source_target_pairs={{0,8},{1,9},{2,10},{3,11},{4,12},{5,13},{6,14},{7,15},{8,0},{9,1},... | collective-permute-start | bytes 196616 | tf_op jit(solution)/shard_map/ppermute | solution.py:33
  33.8 0.8 copy-start.8
  134.8 5.9 %copy-start.17 = (bf16[2048,2048]{1,0:T(8,128)(2,1)S(1)}, bf16[2048,2048]{1,0:T(8,128)(2,1)}, u32[]{:S(2)}) copy-start(bf16[2048,2048]{1,0:T(8,128)(2,1)} %get-tuple-element.7) | copy-start | bytes 25165828
  143.5 0.8 copy-start.2
  143.6 1.0 copy-start.4
  144.4 2.6 %slice-start = ((s8[8388608]{0:T(1024)(128)(4,1)}), s8[4194304]{0:T(1024)(128)(4,1)S(1)}, s32[]{:S(2)}) async-start(s8[8388608]{0:T(1024)(128)(4,1)} %bitcast.232), calls=%async_computation.1 | async-start | bytes 8388608
  144.5 3.3 %slice-start.1 = ((s8[8388608]{0:T(1024)(128)(4,1)}), s8[4194304]{0:T(1024)(128)(4,1)S(1)}, s32[]{:S(2)}) async-start(s8[8388608]{0:T(1024)(128)(4,1)} %bitcast.232), calls=%async_computation.2 | async-start | bytes 8388608
  204.4 1.0 copy-start.3
  204.4 1.2 copy-start.5
  205.6 1.9 copy-start.7
  205.6 1.9 copy-start.9
  205.6 1.9 copy-start.10
  207.8 1.5 copy-start.1
  (5 other events, 3.9 us)
Sparse Core Ops, SparseCore 0:
  34.8 80.8 all-gather.2

commit v5 on v4

--- a/solution.py
+++ b/solution.py
@@ -21,20 +21,19 @@
 
 def upper_blocks(data_field, station_weight, parts, here):
     rows = data_field.shape[1]
-    own_weight = lax.dynamic_slice_in_dim(station_weight, here * rows, rows)
-    blocks = []
-    for s in range(parts // 2 + 1):
-        col = ((here + s) % parts) * rows
-        own = lax.dynamic_slice_in_dim(data_field, col, rows, axis=2)
-        if s == 0:
-            mirror = own.swapaxes(1, 2)
-        else:
-            send = lax.dynamic_slice_in_dim(data_field, ((here - s) % parts) * rows, rows, axis=2)
-            recv = lax.ppermute(send, AXES, perm=[(c, (c - s) % parts) for c in range(parts)])
-            mirror = recv.swapaxes(1, 2)
-        col_weight = lax.dynamic_slice_in_dim(station_weight, col, rows)
-        blocks.append(blend_rows(own, mirror, own_weight, col_weight))
-    return jnp.stack(blocks)
+    half = parts // 2
+    rolled = jnp.roll(data_field.reshape(2, rows, parts, rows), -here, axis=2)
+    own = rolled[:, :, : half + 1]
+    received = [rolled[:, :, 0]]
+    for s in range(1, half + 1):
+        perm = [(c, (c - s) % parts) for c in range(parts)]
+        received.append(lax.ppermute(rolled[:, :, parts - s], AXES, perm=perm))
+    mirror = jnp.stack(received, axis=2).transpose(0, 3, 2, 1)
+    own_weight = lax.dynamic_slice_in_dim(station_weight, here * rows, rows)[:, None, None]
+    col_weight = jnp.roll(station_weight.reshape(parts, rows), -here, axis=0)[None, : half + 1]
+    top = own_weight * own.astype(jnp.float32) + col_weight * mirror.astype(jnp.float32)
+    blended = (top / (own_weight + col_weight)).astype(jnp.bfloat16)
+    return blended.transpose(2, 0, 1, 3)
 
 
 def assemble(gathered, chips, cores):

time: 220 us -> 221 us (level)
  local copies, waits for them, and re-layouts: 10.4 us -> 16 us
  other arithmetic: 15.8 us -> 12.7 us
    unnamed x49 -> x38, local copies, waits for them, and re-layouts: 7.59 us -> 14 us
    unnamed x9 -> x1, other arithmetic: 5.1 us -> 0.01 us
    ppermute x8, waiting for transfers between devices: 2.37 us -> 0.12 us  [upper_blocks(): received.append(lax.ppermute(rolled[:, :, parts - s], AXES, perm=perm))]
    transpose x0 -> x1, other arithmetic: none -> 2.21 us  [upper_blocks(): return blended.transpose(2, 0, 1, 3)]
where the time goes in v5:
time: 221 us; the launch traced here: 218 us
  waiting for transfers between devices  81 us (37%)
  matrix products  61.6 us (28%)
  Pallas kernels  19.1 us (9%)
  local copies, waits for them, and re-layouts  16 us (7%)
  between operations  14.4 us (7%)
  starting transfers between devices  12.8 us (6%)
  other arithmetic  12.7 us (6%)
    all_gather x1, waiting for transfers between devices, local(): gathered = lax.all_gather(mine, AXES)[None]  80.9 us
    dot_general x12, matrix products, local(): jnp.dot(stacked, operator[1], preferred_element_type=jnp.float32)  32.2 us
    dot_general x12, matrix products, local(): jnp.dot(stacked, operator[0], preferred_element_type=jnp.float32)  29.4 us
    pallas_call x1, Pallas kernels, assemble_pallas(): pl.pallas_call(assemble_kernel, grid=(parts,), in_specs=[pl.BlockSpec(mem...  19.1 us
    unnamed x38, local copies, waits for them, and re-layouts  14 us
    ppermute x8, starting transfers between devices, upper_blocks(): received.append(lax.ppermute(rolled[:, :, parts - s], AXES, perm=perm))  12.7 us
    another operation x12, other arithmetic, local(): current = jnp.stack([real_part, imag_part]).astype(jnp.bfloat16)  5.09 us
  transfers between devices with their start and end apart: 9, of which 2 were waited for; matrix products, arithmetic and copies ran while one was open for 5% of the time, Pallas kernels for 0%

profile of v5, /device:TPU:0, one launch (start us, length us, event | category | flops | bytes accessed | tf_op | source)
XLA Modules:
  0.0 217.6 jit_solution(10537773358711480390)
XLA Ops:
  9.4 5.5 %collective-permute-start = (bf16[2,128,128]{1,2,0:T(8,128)(2,1)}, bf16[2,128,128]{1,2,0:T(8,128)(2,1)}, u32[]{:S(2)}, u32[]{:S(2)}) collective-permute-start(bf16[2,128,128]{1,2,0:T(8,128)(2,1)} %get-tuple-element.39), channel_id=1, source_target_pairs={{0,15},{1,0},{2,1},{3,2},{4,3},{5,4},{6,5},{7,6},{8,7},{9,8},{10,9... | collective-permute-start | bytes 196616 | tf_op jit(solution)/shard_map/ppermute | solution.py:30
  17.6 4.3 %collective-permute-start.5 = (bf16[2,128,128]{1,2,0:T(8,128)(2,1)S(1)}, bf16[2,128,128]{1,2,0:T(8,128)(2,1)S(1)}, u32[]{:S(2)}, u32[]{:S(2)}) collective-permute-start(bf16[2,128,128]{1,2,0:T(8,128)(2,1)S(1)} %get-tuple-element.41), channel_id=1, source_target_pairs={{0,10},{1,11},{2,12},{3,13},{4,14},{5,15},{6,0},{7,1},{8,2},{9,3},... | collective-permute-start | bytes 196616 | tf_op jit(solution)/shard_map/ppermute | solution.py:30
  35.6 80.9 %all-gather.3.cloned.1.call-done = bf16[144,2,128,128]{3,2,1,0:T(8,128)(2,1)} async-done(((bf16[9,2,128,128]{3,2,1,0:T(8,128)(2,1)}), bf16[144,2,128,128]{3,2,1,0:T(8,128)(2,1)}) %all-gather.3.cloned.1.call-update) | async-done | bytes 9437200 | tf_op jit(solution)/shard_map/all_gather | solution.py:121
  116.5 19.1 %shard_map.46 = (bf16[2048,2048]{1,0:T(8,128)(2,1)}, bf16[2048,2048]{1,0:T(8,128)(2,1)}) custom-call(bf16[1,16,9,2,128,128]{5,4,3,2,1,0:T(8,128)(2,1)} %bitcast.181), custom_call_target="tpu_custom_call" | custom-call | tf_op jit(solution)/shard_map/pallas_call | solution.py:98
  135.6 5.9 %convolution_bitcast_fusion = f32[256,2048]{1,0:T(8,128)S(1)} fusion(bf16[256,2048]{1,0:T(8,128)(2,1)S(1)} %bitcast.179, bf16[2048,2048]{1,0:T(8,128)(2,1)} %get-tuple-element.8), kind=kOutput, calls=%fused_computation | convolution fusion | flops 2147483648 | bytes 11534336 | tf_op jit(solution)/shard_map/dot_general | solution.py:132
  141.5 2.4 %convolution_bitcast_fusion.1 = f32[256,2048]{1,0:T(8,128)S(1)} fusion(bf16[256,2048]{1,0:T(8,128)(2,1)S(1)} %bitcast.180, bf16[2048,2048]{1,0:T(8,128)(2,1)S(1)} %copy-done.11), kind=kOutput, calls=%fused_computation.1 | convolution fusion | flops 2147483648 | bytes 11534336 | tf_op jit(solution)/shard_map/dot_general | solution.py:131
  151.6 2.4 %fusion.60 = f32[256,2048]{1,0:T(8,128)S(1)} fusion(bf16[256,2048]{1,0:T(8,128)(2,1)S(1)} %bitcast.187, bf16[2048,2048]{1,0:T(8,128)(2,1)S(1)} %copy-done.11), kind=kOutput, calls=%fused_computation.124 | convolution fusion | flops 2147483648 | bytes 11534336 | tf_op jit(solution)/shard_map/dot_general | solution.py:131
  154.0 2.4 %fusion.61 = f32[256,2048]{1,0:T(8,128)S(1)} fusion(bf16[256,2048]{1,0:T(8,128)(2,1)S(1)} %bitcast.188, bf16[2048,2048]{1,0:T(8,128)(2,1)S(1)} %bitcast.209), kind=kOutput, calls=%fused_computation.125 | convolution fusion | flops 2147483648 | bytes 11534336 | tf_op jit(solution)/shard_map/dot_general | solution.py:132
  156.9 2.6 %fusion.62 = f32[256,2048]{1,0:T(8,128)S(1)} fusion(bf16[256,2048]{1,0:T(8,128)(2,1)S(1)} %bitcast.189, bf16[2048,2048]{1,0:T(8,128)(2,1)S(1)} %copy-done.11), kind=kOutput, calls=%fused_computation.126 | convolution fusion | flops 2147483648 | bytes 11534336 | tf_op jit(solution)/shard_map/dot_general | solution.py:131
  159.5 2.4 %fusion.63 = f32[256,2048]{1,0:T(8,128)S(1)} fusion(bf16[256,2048]{1,0:T(8,128)(2,1)S(1)} %bitcast.190, bf16[2048,2048]{1,0:T(8,128)(2,1)S(1)} %bitcast.209), kind=kOutput, calls=%fused_computation.127 | convolution fusion | flops 2147483648 | bytes 11534336 | tf_op jit(solution)/shard_map/dot_general | solution.py:132
  162.5 2.4 %fusion.64 = f32[256,2048]{1,0:T(8,128)S(1)} fusion(bf16[256,2048]{1,0:T(8,128)(2,1)S(1)} %bitcast.191, bf16[2048,2048]{1,0:T(8,128)(2,1)S(1)} %copy-done.11), kind=kOutput, calls=%fused_computation.128 | convolution fusion | flops 2147483648 | bytes 11534336 | tf_op jit(solution)/shard_map/dot_general | solution.py:131
  164.9 2.4 %fusion.65 = f32[256,2048]{1,0:T(8,128)S(1)} fusion(bf16[256,2048]{1,0:T(8,128)(2,1)S(1)} %bitcast.192, bf16[2048,2048]{1,0:T(8,128)(2,1)S(1)} %bitcast.209), kind=kOutput, calls=%fused_computation.129 | convolution fusion | flops 2147483648 | bytes 11534336 | tf_op jit(solution)/shard_map/dot_general | solution.py:132
  167.8 2.4 %fusion.66 = f32[256,2048]{1,0:T(8,128)S(1)} fusion(bf16[256,2048]{1,0:T(8,128)(2,1)S(1)} %bitcast.193, bf16[2048,2048]{1,0:T(8,128)(2,1)S(1)} %copy-done.11), kind=kOutput, calls=%fused_computation.130 | convolution fusion | flops 2147483648 | bytes 11534336 | tf_op jit(solution)/shard_map/dot_general | solution.py:131
  170.2 2.4 %fusion.67 = f32[256,2048]{1,0:T(8,128)S(1)} fusion(bf16[256,2048]{1,0:T(8,128)(2,1)S(1)} %bitcast.194, bf16[2048,2048]{1,0:T(8,128)(2,1)S(1)} %bitcast.209), kind=kOutput, calls=%fused_computation.131 | convolution fusion | flops 2147483648 | bytes 11534336 | tf_op jit(solution)/shard_map/dot_general | solution.py:132
  173.2 2.6 %fusion.68 = f32[256,2048]{1,0:T(8,128)S(1)} fusion(bf16[256,2048]{1,0:T(8,128)(2,1)S(1)} %bitcast.195, bf16[2048,2048]{1,0:T(8,128)(2,1)S(1)} %copy-done.11), kind=kOutput, calls=%fused_computation.132 | convolution fusion | flops 2147483648 | bytes 11534336 | tf_op jit(solution)/shard_map/dot_general | solution.py:131
  175.8 2.4 %fusion.69 = f32[256,2048]{1,0:T(8,128)S(1)} fusion(bf16[256,2048]{1,0:T(8,128)(2,1)S(1)} %bitcast.196, bf16[2048,2048]{1,0:T(8,128)(2,1)S(1)} %bitcast.209), kind=kOutput, calls=%fused_computation.133 | convolution fusion | flops 2147483648 | bytes 11534336 | tf_op jit(solution)/shard_map/dot_general | solution.py:132
  181.1 2.4 %fusion.71 = f32[256,2048]{1,0:T(8,128)S(1)} fusion(bf16[256,2048]{1,0:T(8,128)(2,1)S(1)} %bitcast.198, bf16[2048,2048]{1,0:T(8,128)(2,1)S(1)} %bitcast.209), kind=kOutput, calls=%fused_computation.135 | convolution fusion | flops 2147483648 | bytes 11534336 | tf_op jit(solution)/shard_map/dot_general | solution.py:132
  184.1 2.4 %fusion.72 = f32[256,2048]{1,0:T(8,128)S(1)} fusion(bf16[256,2048]{1,0:T(8,128)(2,1)S(1)} %bitcast.199, bf16[2048,2048]{1,0:T(8,128)(2,1)S(1)} %copy-done.11), kind=kOutput, calls=%fused_computation.136 | convolution fusion | flops 2147483648 | bytes 11534336 | tf_op jit(solution)/shard_map/dot_general | solution.py:131
  186.5 2.4 %fusion.73 = f32[256,2048]{1,0:T(8,128)S(1)} fusion(bf16[256,2048]{1,0:T(8,128)(2,1)S(1)} %bitcast.200, bf16[2048,2048]{1,0:T(8,128)(2,1)S(1)} %bitcast.209), kind=kOutput, calls=%fused_computation.137 | convolution fusion | flops 2147483648 | bytes 11534336 | tf_op jit(solution)/shard_map/dot_general | solution.py:132
  189.4 2.7 %fusion.74 = f32[256,2048]{1,0:T(8,128)S(1)} fusion(bf16[256,2048]{1,0:T(8,128)(2,1)S(1)} %bitcast.201, bf16[2048,2048]{1,0:T(8,128)(2,1)S(1)} %copy-done.11), kind=kOutput, calls=%fused_computation.138 | convolution fusion | flops 2147483648 | bytes 11534336 | tf_op jit(solution)/shard_map/dot_general | solution.py:131
  192.1 2.4 %fusion.75 = f32[256,2048]{1,0:T(8,128)S(1)} fusion(bf16[256,2048]{1,0:T(8,128)(2,1)S(1)} %bitcast.202, bf16[2048,2048]{1,0:T(8,128)(2,1)S(1)} %bitcast.209), kind=kOutput, calls=%fused_computation.139 | convolution fusion | flops 2147483648 | bytes 11534336 | tf_op jit(solution)/shard_map/dot_general | solution.py:132
  197.4 2.4 %fusion.77 = f32[256,2048]{1,0:T(8,128)S(1)} fusion(bf16[256,2048]{1,0:T(8,128)(2,1)S(1)} %bitcast.204, bf16[2048,2048]{1,0:T(8,128)(2,1)S(1)} %bitcast.209), kind=kOutput, calls=%fused_computation.141 | convolution fusion | flops 2147483648 | bytes 11534336 | tf_op jit(solution)/shard_map/dot_general | solution.py:132
  200.3 2.4 %fusion.78 = f32[256,2048]{1,0:T(8,128)S(1)} fusion(bf16[256,2048]{1,0:T(8,128)(2,1)S(1)} %bitcast.183, bf16[2048,2048]{1,0:T(8,128)(2,1)S(1)} %copy-done.11), kind=kOutput, calls=%fused_computation.142 | convolution fusion | flops 2147483648 | bytes 11534336 | tf_op jit(solution)/shard_map/dot_general | solution.py:131
  202.7 2.4 %fusion.79 = f32[256,2048]{1,0:T(8,128)S(1)} fusion(bf16[256,2048]{1,0:T(8,128)(2,1)S(1)} %bitcast.184, bf16[2048,2048]{1,0:T(8,128)(2,1)S(1)} %bitcast.209), kind=kOutput, calls=%fused_computation.143 | convolution fusion | flops 2147483648 | bytes 11534336 | tf_op jit(solution)/shard_map/dot_general | solution.py:132
  (94 shorter events, 41.4 us)
Async XLA Ops:
  6.5 129.1 %copy-start = (bf16[2,128,2048]{2,1,0:T(8,128)(2,1)S(1)}, bf16[2,128,2048]{2,1,0:T(8,128)(2,1)}, u32[]{:S(2)}) copy-start(bf16[2,128,2048]{2,1,0:T(8,128)(2,1)} %param.5) | copy-start | bytes 3145732
  6.5 110.0 %all-gather.3.cloned.1.call-start = ((), (), s32[]{:S(2)}) async-start(), calls=%async_computation | async-start | bytes 10027008 | tf_op jit(solution)/shard_map/all_gather | solution.py:121
  8.2 8.0 %copy-start.10 = (f32[2048]{0:T(1024)S(1)}, f32[2048]{0:T(1024)}, u32[]{:S(2)}) copy-start(f32[2048]{0:T(1024)} %param.6) | copy-start | bytes 24580
  9.4 8.2 %collective-permute-start = (bf16[2,128,128]{1,2,0:T(8,128)(2,1)}, bf16[2,128,128]{1,2,0:T(8,128)(2,1)}, u32[]{:S(2)}, u32[]{:S(2)}) collective-permute-start(bf16[2,128,128]{1,2,0:T(8,128)(2,1)} %get-tuple-element.39), channel_id=1, source_target_pairs={{0,15},{1,0},{2,1},{3,2},{4,3},{5,4},{6,5},{7,6},{8,7},{9,8},{10,9... | collective-permute-start | bytes 196616 | tf_op jit(solution)/shard_map/ppermute | solution.py:30
  14.9 8.5 %collective-permute-start.1 = (bf16[2,128,128]{1,2,0:T(8,128)(2,1)}, bf16[2,128,128]{1,2,0:T(8,128)(2,1)}, u32[]{:S(2)}, u32[]{:S(2)}) collective-permute-start(bf16[2,128,128]{1,2,0:T(8,128)(2,1)} %get-tuple-element.38), channel_id=1, source_target_pairs={{0,14},{1,15},{2,0},{3,1},{4,2},{5,3},{6,4},{7,5},{8,6},{9,7},{10,... | collective-permute-start | bytes 196616 | tf_op jit(solution)/shard_map/ppermute | solution.py:30
  15.4 9.4 %collective-permute-start.2 = (bf16[2,128,128]{1,2,0:T(8,128)(2,1)}, bf16[2,128,128]{1,2,0:T(8,128)(2,1)}, u32[]{:S(2)}, u32[]{:S(2)}) collective-permute-start(bf16[2,128,128]{1,2,0:T(8,128)(2,1)} %get-tuple-element.37), channel_id=1, source_target_pairs={{0,13},{1,14},{2,15},{3,0},{4,1},{5,2},{6,3},{7,4},{8,5},{9,6},{10... | collective-permute-start | bytes 196616 | tf_op jit(solution)/shard_map/ppermute | solution.py:30
  15.7 12.2 %collective-permute-start.3 = (bf16[2,128,128]{1,2,0:T(8,128)(2,1)}, bf16[2,128,128]{1,2,0:T(8,128)(2,1)}, u32[]{:S(2)}, u32[]{:S(2)}) collective-permute-start(bf16[2,128,128]{1,2,0:T(8,128)(2,1)} %get-tuple-element.36), channel_id=1, source_target_pairs={{0,12},{1,13},{2,14},{3,15},{4,0},{5,1},{6,2},{7,3},{8,4},{9,5},{1... | collective-permute-start | bytes 196616 | tf_op jit(solution)/shard_map/ppermute | solution.py:30
  16.2 13.2 %collective-permute-start.4 = (bf16[2,128,128]{1,2,0:T(8,128)(2,1)S(1)}, bf16[2,128,128]{1,2,0:T(8,128)(2,1)}, u32[]{:S(2)}, u32[]{:S(2)}) collective-permute-start(bf16[2,128,128]{1,2,0:T(8,128)(2,1)S(1)} %get-tuple-element.42), channel_id=1, source_target_pairs={{0,11},{1,12},{2,13},{3,14},{4,15},{5,0},{6,1},{7,2},{8,3},{9,4},{... | collective-permute-start | bytes 196616 | tf_op jit(solution)/shard_map/ppermute | solution.py:30
  17.4 17.6 %copy-start.9 = (f32[2,2048]{1,0:T(2,128)S(1)}, f32[2,2048]{1,0:T(2,128)}, u32[]{:S(2)}) copy-start(f32[2,2048]{1,0:T(2,128)} %param.7) | copy-start | bytes 49156
  17.6 13.3 %collective-permute-start.5 = (bf16[2,128,128]{1,2,0:T(8,128)(2,1)S(1)}, bf16[2,128,128]{1,2,0:T(8,128)(2,1)S(1)}, u32[]{:S(2)}, u32[]{:S(2)}) collective-permute-start(bf16[2,128,128]{1,2,0:T(8,128)(2,1)S(1)} %get-tuple-element.41), channel_id=1, source_target_pairs={{0,10},{1,11},{2,12},{3,13},{4,14},{5,15},{6,0},{7,1},{8,2},{9,3},... | collective-permute-start | bytes 196616 | tf_op jit(solution)/shard_map/ppermute | solution.py:30
  23.4 8.1 %collective-permute-start.6 = (bf16[2,128,128]{1,2,0:T(8,128)(2,1)S(1)}, bf16[2,128,128]{1,2,0:T(8,128)(2,1)S(1)}, u32[]{:S(2)}, u32[]{:S(2)}) collective-permute-start(bf16[2,128,128]{1,2,0:T(8,128)(2,1)S(1)} %get-tuple-element.40), channel_id=1, source_target_pairs={{0,9},{1,10},{2,11},{3,12},{4,13},{5,14},{6,15},{7,0},{8,1},{9,2},... | collective-permute-start | bytes 196616 | tf_op jit(solution)/shard_map/ppermute | solution.py:30
  24.9 7.3 %collective-permute-start.7 = (bf16[2,128,128]{1,2,0:T(8,128)(2,1)S(1)}, bf16[2,128,128]{1,2,0:T(8,128)(2,1)S(1)}, u32[]{:S(2)}, u32[]{:S(2)}) collective-permute-start(bf16[2,128,128]{1,2,0:T(8,128)(2,1)S(1)} %get-tuple-element.35), channel_id=1, source_target_pairs={{0,8},{1,9},{2,10},{3,11},{4,12},{5,13},{6,14},{7,15},{8,0},{9,1},... | collective-permute-start | bytes 196616 | tf_op jit(solution)/shard_map/ppermute | solution.py:30
  135.6 5.9 %copy-start.11 = (bf16[2048,2048]{1,0:T(8,128)(2,1)S(1)}, bf16[2048,2048]{1,0:T(8,128)(2,1)}, u32[]{:S(2)}) copy-start(bf16[2048,2048]{1,0:T(8,128)(2,1)} %get-tuple-element.7) | copy-start | bytes 25165828
  144.4 0.8 copy-start.2
  144.4 1.0 copy-start.4
  145.2 2.6 %slice-start = ((s8[8388608]{0:T(1024)(128)(4,1)}), s8[4194304]{0:T(1024)(128)(4,1)S(1)}, s32[]{:S(2)}) async-start(s8[8388608]{0:T(1024)(128)(4,1)} %bitcast.208), calls=%async_computation.1 | async-start | bytes 8388608
  145.3 3.3 %slice-start.1 = ((s8[8388608]{0:T(1024)(128)(4,1)}), s8[4194304]{0:T(1024)(128)(4,1)S(1)}, s32[]{:S(2)}) async-start(s8[8388608]{0:T(1024)(128)(4,1)} %bitcast.208), calls=%async_computation.2 | async-start | bytes 8388608
  205.2 1.0 copy-start.3
  205.2 1.2 copy-start.5
  206.4 1.9 copy-start.6
  206.4 1.9 copy-start.7
  206.4 2.0 copy-start.8
  208.7 1.6 copy-start.1
Sparse Core Ops, SparseCore 0:
  35.1 81.3 all-gather.2

commit v6 on v5

--- a/solution.py
+++ b/solution.py
@@ -28,12 +28,20 @@
     for s in range(1, half + 1):
         perm = [(c, (c - s) % parts) for c in range(parts)]
         received.append(lax.ppermute(rolled[:, :, parts - s], AXES, perm=perm))
-    mirror = jnp.stack(received, axis=2).transpose(0, 3, 2, 1)
     own_weight = lax.dynamic_slice_in_dim(station_weight, here * rows, rows)[:, None, None]
     col_weight = jnp.roll(station_weight.reshape(parts, rows), -here, axis=0)[None, : half + 1]
-    top = own_weight * own.astype(jnp.float32) + col_weight * mirror.astype(jnp.float32)
-    blended = (top / (own_weight + col_weight)).astype(jnp.bfloat16)
-    return blended.transpose(2, 0, 1, 3)
+    chunks = []
+    for lo, hi in chunk_bounds(half + 1):
+        mirror = jnp.stack(received[lo:hi], axis=2).transpose(0, 3, 2, 1)
+        top = own_weight * own[:, :, lo:hi].astype(jnp.float32) + col_weight[:, lo:hi] * mirror.astype(jnp.float32)
+        blended = (top / (own_weight + col_weight[:, lo:hi])).astype(jnp.bfloat16)
+        chunks.append(blended.transpose(2, 0, 1, 3))
+    return chunks
+
+
+def chunk_bounds(slots, pieces=3):
+    edges = [round(i * slots / pieces) for i in range(pieces + 1)]
+    return list(zip(edges[:-1], edges[1:]))
 
 
 def assemble(gathered, chips, cores):
@@ -56,16 +64,23 @@
     return blocks.transpose(2, 0, 3, 1, 4).reshape(2, parts * rows, parts * rows)
 
 
-def assemble_kernel(g_ref, re_ref, im_ref, upper, lower, sem):
-    cores, chips, slots, _, rows, _ = g_ref.shape
-    parts = chips * cores
+def assemble_kernel(*refs):
+    pieces = len(refs) - 5
+    g_refs, (re_ref, im_ref, upper, lower, sem) = refs[:pieces], refs[pieces:]
+    parts = g_refs[0].shape[0]
+    rows = g_refs[0].shape[-1]
+    bounds = chunk_bounds(parts // 2 + 1, pieces)
     r = pl.program_id(0)
 
     def copies(row, slot):
-        out = [pltpu.make_async_copy(g_ref.at[row % cores, row // cores], upper.at[slot], sem.at[slot, 0])]
+        out = []
+        for k, (lo, hi) in enumerate(bounds):
+            out.append(pltpu.make_async_copy(g_refs[k].at[row], upper.at[slot, pl.ds(lo, hi - lo)], sem.at[slot, k]))
         for t in range(1, parts // 2):
             a = (row + parts - t) % parts
-            out.append(pltpu.make_async_copy(g_ref.at[a % cores, a // cores, t], lower.at[slot, t], sem.at[slot, t]))
+            k = [k for k, (lo, hi) in enumerate(bounds) if lo <= t < hi][0]
+            src = g_refs[k].at[a, t - bounds[k][0]]
+            out.append(pltpu.make_async_copy(src, lower.at[slot, t], sem.at[slot, pieces + t]))
         return out
 
     @pl.when(r == 0)
@@ -91,23 +106,24 @@
             out[:, pl.ds(col, rows)] = block
 
 
-def assemble_pallas(gathered, chips, cores):
-    parts = chips * cores
-    rows = gathered.shape[-1]
+def assemble_pallas(chunks):
+    parts = chunks[0].shape[0]
+    rows = chunks[0].shape[-1]
+    slots = sum(c.shape[1] for c in chunks)
     order = parts * rows
     return pl.pallas_call(
         assemble_kernel,
         grid=(parts,),
-        in_specs=[pl.BlockSpec(memory_space=pl.ANY)],
+        in_specs=[pl.BlockSpec(memory_space=pl.ANY)] * len(chunks),
         out_specs=[pl.BlockSpec((rows, order), lambda r: (r, 0))] * 2,
         out_shape=[jax.ShapeDtypeStruct((order, order), jnp.bfloat16)] * 2,
         scratch_shapes=[
-            pltpu.VMEM((2, gathered.shape[2], 2, rows, rows), jnp.bfloat16),
+            pltpu.VMEM((2, slots, 2, rows, rows), jnp.bfloat16),
             pltpu.VMEM((2, parts // 2, 2, rows, rows), jnp.bfloat16),
-            pltpu.SemaphoreType.DMA((2, parts // 2)),
+            pltpu.SemaphoreType.DMA((2, len(chunks) + parts // 2)),
         ],
         compiler_params=pltpu.CompilerParams(dimension_semantics=("arbitrary",)),
-    )(gathered)
+    )(*chunks)
 
 
 def local(data_field, primary_field, station_weight, adaptive_filter):
@@ -117,23 +133,25 @@
     cores = lax.axis_size("core")
     parts = chips * cores
     here = lax.axis_index("chip") * cores + lax.axis_index("core")
-    mine = upper_blocks(data_field, station_weight, parts, here)
-    gathered = lax.all_gather(mine, AXES)[None]
+    pieces = upper_blocks(data_field, station_weight, parts, here)
+    gathered = [lax.all_gather(jnp.concatenate(pieces, axis=0), AXES)]
     if rows % 128 == 0:
-        operator = assemble_pallas(gathered, parts, 1)
+        operator = assemble_pallas(gathered)
     else:
-        operator = assemble(gathered, parts, 1)
+        operator = assemble(jnp.concatenate(gathered, axis=1)[None], parts, 1)
     factor = 0.8 / math.sqrt(order)
-    current = primary_field
-    prediction = jnp.zeros(data_field.shape, jnp.float32)
-    for step in range(ORDERS):
+
+    def step(_, carry):
+        current, prediction = carry
         stacked = current.reshape(2 * rows, order)
         with_real = jnp.dot(stacked, operator[0], preferred_element_type=jnp.float32)
         with_imag = jnp.dot(stacked, operator[1], preferred_element_type=jnp.float32)
         real_part = (with_real[:rows] - with_imag[rows:]) * factor
         imag_part = (with_imag[:rows] + with_real[rows:]) * factor
         current = jnp.stack([real_part, imag_part]).astype(jnp.bfloat16)
-        prediction = prediction + current.astype(jnp.float32)
+        return current, prediction + current.astype(jnp.float32)
+
+    current, prediction = lax.fori_loop(0, ORDERS, step, (primary_field, jnp.zeros(data_field.shape, jnp.float32)))
     filt_re = adaptive_filter[0][None, :]
     filt_im = adaptive_filter[1][None, :]
     out_re = data_field[0].astype(jnp.float32) - (filt_re * prediction[0] - filt_im * prediction[1])

time: 221 us -> 288 us (1.30)
  matrix products: 61.6 us -> 118 us
  other arithmetic: 12.7 us -> 30.1 us
  local copies, waits for them, and re-layouts: 16 us -> 3.82 us
  waiting for transfers between devices: 81 us -> 87.6 us
    dot_general x24, matrix products: 61.6 us -> 118 us  [the longest x12 74.1 us: step(): jnp.dot(stacked, operator[1], preferred_element_type=jnp.float32)]
    add x2 -> x13, other arithmetic: 2.04 us -> 20.3 us  [the longest x12 20.2 us: step(): return (current, prediction + current.astype(jnp.float32))]
    unnamed x38 -> x12, local copies, waits for them, and re-layouts: 14 us -> 3.63 us
    ppermute x8, waiting for transfers between devices: 0.12 us -> 4.1 us  [upper_blocks(): received.append(lax.ppermute(rolled[:, :, parts - s], AXES, perm=perm))]
  transfers between devices with their start and end apart: 9 -> 9, of which waited for: 2 -> 2; matrix products, arithmetic and copies ran while one was open for 5% -> 0% of each run, Pallas kernels for 0% -> 0%
where the time goes in v6:
time: 288 us; the launch traced here: 287 us
  matrix products  118 us (41%)
  waiting for transfers between devices  87.6 us (30%)
  other arithmetic  30.1 us (10%)
  Pallas kernels  18.7 us (6%)
  starting transfers between devices  15.2 us (5%)
  between operations  13.6 us (5%)
  local copies, waits for them, and re-layouts  3.82 us (1%)
    all_gather x1, waiting for transfers between devices, local(): gathered = [lax.all_gather(jnp.concatenate(pieces, axis=0), AXES)]  83.5 us
    dot_general x12, matrix products, step(): jnp.dot(stacked, operator[1], preferred_element_type=jnp.float32)  74.1 us
    dot_general x12, matrix products, step(): jnp.dot(stacked, operator[0], preferred_element_type=jnp.float32)  43.7 us
    add x12, other arithmetic, step(): return (current, prediction + current.astype(jnp.float32))  20.2 us
    pallas_call x1, Pallas kernels, assemble_pallas(): pl.pallas_call(assemble_kernel, grid=(parts,), in_specs=[pl.BlockSpec(mem...  18.7 us
    ppermute x8, starting transfers between devices, upper_blocks(): received.append(lax.ppermute(rolled[:, :, parts - s], AXES, perm=perm))  15.2 us
  transfers between devices with their start and end apart: 9, of which 2 were waited for; matrix products, arithmetic and copies ran while one was open for 0% of the time, Pallas kernels for 0%

profile of v6, /device:TPU:0, one launch (start us, length us, event | category | flops | bytes accessed | tf_op | source)
XLA Modules:
  0.0 287.2 jit_solution(3252759596422444776)
XLA Ops:
  10.1 4.6 %collective-permute-start.2 = (bf16[2,128,128]{1,2,0:T(8,128)(2,1)S(1)}, bf16[2,128,128]{1,2,0:T(8,128)(2,1)S(1)}, u32[]{:S(2)}, u32[]{:S(2)}) collective-permute-start(bf16[2,128,128]{1,2,0:T(8,128)(2,1)S(1)} %get-tuple-element.77), channel_id=1, source_target_pairs={{0,13},{1,14},{2,15},{3,0},{4,1},{5,2},{6,3},{7,4},{8,5},{9,6},{10... | collective-permute-start | bytes 196616 | tf_op jit(solution)/shard_map/ppermute | solution.py:30
  15.5 4.4 %collective-permute-start.5 = (bf16[2,128,128]{1,2,0:T(8,128)(2,1)S(1)}, bf16[2,128,128]{1,2,0:T(8,128)(2,1)S(1)}, u32[]{:S(2)}, u32[]{:S(2)}) collective-permute-start(bf16[2,128,128]{1,2,0:T(8,128)(2,1)S(1)} %get-tuple-element.82), channel_id=1, source_target_pairs={{0,10},{1,11},{2,12},{3,13},{4,14},{5,15},{6,0},{7,1},{8,2},{9,3},... | collective-permute-start | bytes 196616 | tf_op jit(solution)/shard_map/ppermute | solution.py:30
  26.1 4.1 %collective-permute-done.7 = bf16[2,128,128]{1,2,0:T(8,128)(2,1)S(1)} collective-permute-done((bf16[2,128,128]{1,2,0:T(8,128)(2,1)S(1)}, bf16[2,128,128]{1,2,0:T(8,128)(2,1)S(1)}, u32[]{:S(2)}, u32[]{:S(2)}) %collective-permute-start.7) | collective-permute-done | bytes 65568 | tf_op jit(solution)/shard_map/ppermute | solution.py:30
  31.5 83.5 %all-gather.3.cloned.1.call-done = bf16[144,2,128,128]{3,2,1,0:T(8,128)(2,1)} async-done(((bf16[9,2,128,128]{3,2,1,0:T(8,128)(2,1)}), bf16[144,2,128,128]{3,2,1,0:T(8,128)(2,1)}) %all-gather.3.cloned.1.call-update) | async-done | bytes 9437200 | tf_op jit(solution)/shard_map/all_gather | solution.py:137
  115.0 18.7 %shard_map.46 = (bf16[2048,2048]{1,0:T(8,128)(2,1)}, bf16[2048,2048]{1,0:T(8,128)(2,1)}) custom-call(bf16[16,9,2,128,128]{4,3,2,1,0:T(8,128)(2,1)} %bitcast.110), custom_call_target="tpu_custom_call" | custom-call | tf_op jit(solution)/shard_map/pallas_call | solution.py:114
  133.7 143.6 %while.13 = (s32[]{:T(128)}, bf16[2,128,2048]{2,1,0:T(8,128)(2,1)}, f32[2,128,2048]{2,1,0:T(8,128)S(1)}, bf16[2048,2048]{1,0:T(8,128)(2,1)}, bf16[2048,2048]{1,0:T(8,128)(2,1)}, /*index=5*/s32[]{:T(128)}, s32[]{:T(128)}) while((s32[]{:T(128)}, bf16[2,128,2048]{2,1,0:T(8,128)(2,1)}, f32[2,128,2048]{2,1,0:T(8,128)S(1)}, ...), condition=%wide.region_1.2_spmd.clone, body=%wide.region_0.1_spmd.clone.sunk | while | flops 4298637312 | bytes 68157552 | solution.py:154
  133.7 6.2 %fusion.40 = f32[256,2048]{1,0:T(8,128)S(1)} fusion(bf16[256,2048]{1,0:T(8,128)(2,1)} %bitcast.109, bf16[2048,2048]{1,0:T(8,128)(2,1)} %get-tuple-element.151), kind=kOutput, calls=%fused_computation.54.clone.1 | convolution fusion | flops 2147483648 | bytes 11534336 | tf_op jit(solution)/shard_map/while/body/eval_jaxpr/dot_general | solution.py:148
  139.9 3.6 %fusion.41 = f32[256,2048]{1,0:T(8,128)S(1)} fusion(bf16[256,2048]{1,0:T(8,128)(2,1)} %bitcast.109, bf16[2048,2048]{1,0:T(8,128)(2,1)S(1)} %copy-done.3), kind=kOutput, calls=%fused_computation.53.clone.1 | convolution fusion | flops 2147483648 | bytes 11534336 | tf_op jit(solution)/shard_map/while/body/eval_jaxpr/dot_general | solution.py:147
  145.7 6.2 %fusion.40 = f32[256,2048]{1,0:T(8,128)S(1)} fusion(bf16[256,2048]{1,0:T(8,128)(2,1)} %bitcast.109, bf16[2048,2048]{1,0:T(8,128)(2,1)} %get-tuple-element.151), kind=kOutput, calls=%fused_computation.54.clone.1 | convolution fusion | flops 2147483648 | bytes 11534336 | tf_op jit(solution)/shard_map/while/body/eval_jaxpr/dot_general | solution.py:148
  151.8 3.6 %fusion.41 = f32[256,2048]{1,0:T(8,128)S(1)} fusion(bf16[256,2048]{1,0:T(8,128)(2,1)} %bitcast.109, bf16[2048,2048]{1,0:T(8,128)(2,1)S(1)} %copy-done.3), kind=kOutput, calls=%fused_computation.53.clone.1 | convolution fusion | flops 2147483648 | bytes 11534336 | tf_op jit(solution)/shard_map/while/body/eval_jaxpr/dot_general | solution.py:147
  157.6 6.2 %fusion.40 = f32[256,2048]{1,0:T(8,128)S(1)} fusion(bf16[256,2048]{1,0:T(8,128)(2,1)} %bitcast.109, bf16[2048,2048]{1,0:T(8,128)(2,1)} %get-tuple-element.151), kind=kOutput, calls=%fused_computation.54.clone.1 | convolution fusion | flops 2147483648 | bytes 11534336 | tf_op jit(solution)/shard_map/while/body/eval_jaxpr/dot_general | solution.py:148
  169.6 6.2 %fusion.40 = f32[256,2048]{1,0:T(8,128)S(1)} fusion(bf16[256,2048]{1,0:T(8,128)(2,1)} %bitcast.109, bf16[2048,2048]{1,0:T(8,128)(2,1)} %get-tuple-element.151), kind=kOutput, calls=%fused_computation.54.clone.1 | convolution fusion | flops 2147483648 | bytes 11534336 | tf_op jit(solution)/shard_map/while/body/eval_jaxpr/dot_general | solution.py:148
  181.6 6.2 %fusion.40 = f32[256,2048]{1,0:T(8,128)S(1)} fusion(bf16[256,2048]{1,0:T(8,128)(2,1)} %bitcast.109, bf16[2048,2048]{1,0:T(8,128)(2,1)} %get-tuple-element.151), kind=kOutput, calls=%fused_computation.54.clone.1 | convolution fusion | flops 2147483648 | bytes 11534336 | tf_op jit(solution)/shard_map/while/body/eval_jaxpr/dot_general | solution.py:148
  187.7 3.6 %fusion.41 = f32[256,2048]{1,0:T(8,128)S(1)} fusion(bf16[256,2048]{1,0:T(8,128)(2,1)} %bitcast.109, bf16[2048,2048]{1,0:T(8,128)(2,1)S(1)} %copy-done.3), kind=kOutput, calls=%fused_computation.53.clone.1 | convolution fusion | flops 2147483648 | bytes 11534336 | tf_op jit(solution)/shard_map/while/body/eval_jaxpr/dot_general | solution.py:147
  193.5 6.2 %fusion.40 = f32[256,2048]{1,0:T(8,128)S(1)} fusion(bf16[256,2048]{1,0:T(8,128)(2,1)} %bitcast.109, bf16[2048,2048]{1,0:T(8,128)(2,1)} %get-tuple-element.151), kind=kOutput, calls=%fused_computation.54.clone.1 | convolution fusion | flops 2147483648 | bytes 11534336 | tf_op jit(solution)/shard_map/while/body/eval_jaxpr/dot_general | solution.py:148
  199.7 3.6 %fusion.41 = f32[256,2048]{1,0:T(8,128)S(1)} fusion(bf16[256,2048]{1,0:T(8,128)(2,1)} %bitcast.109, bf16[2048,2048]{1,0:T(8,128)(2,1)S(1)} %copy-done.3), kind=kOutput, calls=%fused_computation.53.clone.1 | convolution fusion | flops 2147483648 | bytes 11534336 | tf_op jit(solution)/shard_map/while/body/eval_jaxpr/dot_general | solution.py:147
  205.5 6.2 %fusion.40 = f32[256,2048]{1,0:T(8,128)S(1)} fusion(bf16[256,2048]{1,0:T(8,128)(2,1)} %bitcast.109, bf16[2048,2048]{1,0:T(8,128)(2,1)} %get-tuple-element.151), kind=kOutput, calls=%fused_computation.54.clone.1 | convolution fusion | flops 2147483648 | bytes 11534336 | tf_op jit(solution)/shard_map/while/body/eval_jaxpr/dot_general | solution.py:148
  217.5 6.2 %fusion.40 = f32[256,2048]{1,0:T(8,128)S(1)} fusion(bf16[256,2048]{1,0:T(8,128)(2,1)} %bitcast.109, bf16[2048,2048]{1,0:T(8,128)(2,1)} %get-tuple-element.151), kind=kOutput, calls=%fused_computation.54.clone.1 | convolution fusion | flops 2147483648 | bytes 11534336 | tf_op jit(solution)/shard_map/while/body/eval_jaxpr/dot_general | solution.py:148
  229.4 6.2 %fusion.40 = f32[256,2048]{1,0:T(8,128)S(1)} fusion(bf16[256,2048]{1,0:T(8,128)(2,1)} %bitcast.109, bf16[2048,2048]{1,0:T(8,128)(2,1)} %get-tuple-element.151), kind=kOutput, calls=%fused_computation.54.clone.1 | convolution fusion | flops 2147483648 | bytes 11534336 | tf_op jit(solution)/shard_map/while/body/eval_jaxpr/dot_general | solution.py:148
  235.6 3.6 %fusion.41 = f32[256,2048]{1,0:T(8,128)S(1)} fusion(bf16[256,2048]{1,0:T(8,128)(2,1)} %bitcast.109, bf16[2048,2048]{1,0:T(8,128)(2,1)S(1)} %copy-done.3), kind=kOutput, calls=%fused_computation.53.clone.1 | convolution fusion | flops 2147483648 | bytes 11534336 | tf_op jit(solution)/shard_map/while/body/eval_jaxpr/dot_general | solution.py:147
  241.4 6.2 %fusion.40 = f32[256,2048]{1,0:T(8,128)S(1)} fusion(bf16[256,2048]{1,0:T(8,128)(2,1)} %bitcast.109, bf16[2048,2048]{1,0:T(8,128)(2,1)} %get-tuple-element.151), kind=kOutput, calls=%fused_computation.54.clone.1 | convolution fusion | flops 2147483648 | bytes 11534336 | tf_op jit(solution)/shard_map/while/body/eval_jaxpr/dot_general | solution.py:148
  247.6 3.6 %fusion.41 = f32[256,2048]{1,0:T(8,128)S(1)} fusion(bf16[256,2048]{1,0:T(8,128)(2,1)} %bitcast.109, bf16[2048,2048]{1,0:T(8,128)(2,1)S(1)} %copy-done.3), kind=kOutput, calls=%fused_computation.53.clone.1 | convolution fusion | flops 2147483648 | bytes 11534336 | tf_op jit(solution)/shard_map/while/body/eval_jaxpr/dot_general | solution.py:147
  253.4 6.2 %fusion.40 = f32[256,2048]{1,0:T(8,128)S(1)} fusion(bf16[256,2048]{1,0:T(8,128)(2,1)} %bitcast.109, bf16[2048,2048]{1,0:T(8,128)(2,1)} %get-tuple-element.151), kind=kOutput, calls=%fused_computation.54.clone.1 | convolution fusion | flops 2147483648 | bytes 11534336 | tf_op jit(solution)/shard_map/while/body/eval_jaxpr/dot_general | solution.py:148
  265.3 6.2 %fusion.40 = f32[256,2048]{1,0:T(8,128)S(1)} fusion(bf16[256,2048]{1,0:T(8,128)(2,1)} %bitcast.109, bf16[2048,2048]{1,0:T(8,128)(2,1)} %get-tuple-element.151), kind=kOutput, calls=%fused_computation.54.clone.1 | convolution fusion | flops 2147483648 | bytes 11534336 | tf_op jit(solution)/shard_map/while/body/eval_jaxpr/dot_general | solution.py:148
  (93 shorter events, 62.0 us)
Async XLA Ops:
  6.5 2.4 copy-start
  6.5 108.4 %all-gather.3.cloned.1.call-start = ((), (), s32[]{:S(2)}) async-start(), calls=%async_computation | async-start | bytes 10027008 | tf_op jit(solution)/shard_map/all_gather | solution.py:137
  9.6 10.4 %copy-start.2 = (f32[2048]{0:T(1024)S(1)}, f32[2048]{0:T(1024)}, u32[]{:S(2)}) copy-start(f32[2048]{0:T(1024)} %param.8) | copy-start | bytes 24580
  10.1 10.1 %collective-permute-start.2 = (bf16[2,128,128]{1,2,0:T(8,128)(2,1)S(1)}, bf16[2,128,128]{1,2,0:T(8,128)(2,1)S(1)}, u32[]{:S(2)}, u32[]{:S(2)}) collective-permute-start(bf16[2,128,128]{1,2,0:T(8,128)(2,1)S(1)} %get-tuple-element.77), channel_id=1, source_target_pairs={{0,13},{1,14},{2,15},{3,0},{4,1},{5,2},{6,3},{7,4},{8,5},{9,6},{10... | collective-permute-start | bytes 196616 | tf_op jit(solution)/shard_map/ppermute | solution.py:30
  14.6 7.0 %collective-permute-start.3 = (bf16[2,128,128]{1,2,0:T(8,128)(2,1)S(1)}, bf16[2,128,128]{1,2,0:T(8,128)(2,1)S(1)}, u32[]{:S(2)}, u32[]{:S(2)}) collective-permute-start(bf16[2,128,128]{1,2,0:T(8,128)(2,1)S(1)} %get-tuple-element.76), channel_id=1, source_target_pairs={{0,12},{1,13},{2,14},{3,15},{4,0},{5,1},{6,2},{7,3},{8,4},{9,5},{1... | collective-permute-start | bytes 196616 | tf_op jit(solution)/shard_map/ppermute | solution.py:30
  15.3 9.6 %collective-permute-start.4 = (bf16[2,128,128]{1,2,0:T(8,128)(2,1)S(1)}, bf16[2,128,128]{1,2,0:T(8,128)(2,1)S(1)}, u32[]{:S(2)}, u32[]{:S(2)}) collective-permute-start(bf16[2,128,128]{1,2,0:T(8,128)(2,1)S(1)} %get-tuple-element.75), channel_id=1, source_target_pairs={{0,11},{1,12},{2,13},{3,14},{4,15},{5,0},{6,1},{7,2},{8,3},{9,4},{... | collective-permute-start | bytes 196616 | tf_op jit(solution)/shard_map/ppermute | solution.py:30
  15.5 10.6 %collective-permute-start.5 = (bf16[2,128,128]{1,2,0:T(8,128)(2,1)S(1)}, bf16[2,128,128]{1,2,0:T(8,128)(2,1)S(1)}, u32[]{:S(2)}, u32[]{:S(2)}) collective-permute-start(bf16[2,128,128]{1,2,0:T(8,128)(2,1)S(1)} %get-tuple-element.82), channel_id=1, source_target_pairs={{0,10},{1,11},{2,12},{3,13},{4,14},{5,15},{6,0},{7,1},{8,2},{9,3},... | collective-permute-start | bytes 196616 | tf_op jit(solution)/shard_map/ppermute | solution.py:30
  20.0 6.1 %collective-permute-start.6 = (bf16[2,128,128]{1,2,0:T(8,128)(2,1)S(1)}, bf16[2,128,128]{1,2,0:T(8,128)(2,1)S(1)}, u32[]{:S(2)}, u32[]{:S(2)}) collective-permute-start(bf16[2,128,128]{1,2,0:T(8,128)(2,1)S(1)} %get-tuple-element.81), channel_id=1, source_target_pairs={{0,9},{1,10},{2,11},{3,12},{4,13},{5,14},{6,15},{7,0},{8,1},{9,2},... | collective-permute-start | bytes 196616 | tf_op jit(solution)/shard_map/ppermute | solution.py:30
  20.2 10.0 %collective-permute-start.7 = (bf16[2,128,128]{1,2,0:T(8,128)(2,1)S(1)}, bf16[2,128,128]{1,2,0:T(8,128)(2,1)S(1)}, u32[]{:S(2)}, u32[]{:S(2)}) collective-permute-start(bf16[2,128,128]{1,2,0:T(8,128)(2,1)S(1)} %get-tuple-element.80), channel_id=1, source_target_pairs={{0,8},{1,9},{2,10},{3,11},{4,12},{5,13},{6,14},{7,15},{8,0},{9,1},... | collective-permute-start | bytes 196616 | tf_op jit(solution)/shard_map/ppermute | solution.py:30
  21.7 8.5 %collective-permute-start = (bf16[2,128,128]{1,2,0:T(8,128)(2,1)S(1)}, bf16[2,128,128]{1,2,0:T(8,128)(2,1)S(1)}, u32[]{:S(2)}, u32[]{:S(2)}) collective-permute-start(bf16[2,128,128]{1,2,0:T(8,128)(2,1)S(1)} %get-tuple-element.79), channel_id=1, source_target_pairs={{0,15},{1,0},{2,1},{3,2},{4,3},{5,4},{6,5},{7,6},{8,7},{9,8},{10,9... | collective-permute-start | bytes 196616 | tf_op jit(solution)/shard_map/ppermute | solution.py:30
  24.9 5.3 %collective-permute-start.1 = (bf16[2,128,128]{1,2,0:T(8,128)(2,1)S(1)}, bf16[2,128,128]{1,2,0:T(8,128)(2,1)S(1)}, u32[]{:S(2)}, u32[]{:S(2)}) collective-permute-start(bf16[2,128,128]{1,2,0:T(8,128)(2,1)S(1)} %get-tuple-element.78), channel_id=1, source_target_pairs={{0,14},{1,15},{2,0},{3,1},{4,2},{5,3},{6,4},{7,5},{8,6},{9,7},{10,... | collective-permute-start | bytes 196616 | tf_op jit(solution)/shard_map/ppermute | solution.py:30
  26.1 5.4 %copy-start.1 = (f32[2,2048]{1,0:T(2,128)S(1)}, f32[2,2048]{1,0:T(2,128)}, u32[]{:S(2)}) copy-start(f32[2,2048]{1,0:T(2,128)} %param.9) | copy-start | bytes 49156
  133.7 6.2 %copy-start.3 = (bf16[2048,2048]{1,0:T(8,128)(2,1)S(1)}, bf16[2048,2048]{1,0:T(8,128)(2,1)}, u32[]{:S(2)}) copy-start(bf16[2048,2048]{1,0:T(8,128)(2,1)} %get-tuple-element.150) | copy-start | bytes 25165828 | tf_op jit(solution)/shard_map/while
  145.7 6.2 %copy-start.3 = (bf16[2048,2048]{1,0:T(8,128)(2,1)S(1)}, bf16[2048,2048]{1,0:T(8,128)(2,1)}, u32[]{:S(2)}) copy-start(bf16[2048,2048]{1,0:T(8,128)(2,1)} %get-tuple-element.150) | copy-start | bytes 25165828 | tf_op jit(solution)/shard_map/while
  157.6 6.2 %copy-start.3 = (bf16[2048,2048]{1,0:T(8,128)(2,1)S(1)}, bf16[2048,2048]{1,0:T(8,128)(2,1)}, u32[]{:S(2)}) copy-start(bf16[2048,2048]{1,0:T(8,128)(2,1)} %get-tuple-element.150) | copy-start | bytes 25165828 | tf_op jit(solution)/shard_map/while
  169.6 6.2 %copy-start.3 = (bf16[2048,2048]{1,0:T(8,128)(2,1)S(1)}, bf16[2048,2048]{1,0:T(8,128)(2,1)}, u32[]{:S(2)}) copy-start(bf16[2048,2048]{1,0:T(8,128)(2,1)} %get-tuple-element.150) | copy-start | bytes 25165828 | tf_op jit(solution)/shard_map/while
  181.6 6.2 %copy-start.3 = (bf16[2048,2048]{1,0:T(8,128)(2,1)S(1)}, bf16[2048,2048]{1,0:T(8,128)(2,1)}, u32[]{:S(2)}) copy-start(bf16[2048,2048]{1,0:T(8,128)(2,1)} %get-tuple-element.150) | copy-start | bytes 25165828 | tf_op jit(solution)/shard_map/while
  193.5 6.2 %copy-start.3 = (bf16[2048,2048]{1,0:T(8,128)(2,1)S(1)}, bf16[2048,2048]{1,0:T(8,128)(2,1)}, u32[]{:S(2)}) copy-start(bf16[2048,2048]{1,0:T(8,128)(2,1)} %get-tuple-element.150) | copy-start | bytes 25165828 | tf_op jit(solution)/shard_map/while
  205.5 6.2 %copy-start.3 = (bf16[2048,2048]{1,0:T(8,128)(2,1)S(1)}, bf16[2048,2048]{1,0:T(8,128)(2,1)}, u32[]{:S(2)}) copy-start(bf16[2048,2048]{1,0:T(8,128)(2,1)} %get-tuple-element.150) | copy-start | bytes 25165828 | tf_op jit(solution)/shard_map/while
  217.5 6.2 %copy-start.3 = (bf16[2048,2048]{1,0:T(8,128)(2,1)S(1)}, bf16[2048,2048]{1,0:T(8,128)(2,1)}, u32[]{:S(2)}) copy-start(bf16[2048,2048]{1,0:T(8,128)(2,1)} %get-tuple-element.150) | copy-start | bytes 25165828 | tf_op jit(solution)/shard_map/while
  229.4 6.2 %copy-start.3 = (bf16[2048,2048]{1,0:T(8,128)(2,1)S(1)}, bf16[2048,2048]{1,0:T(8,128)(2,1)}, u32[]{:S(2)}) copy-start(bf16[2048,2048]{1,0:T(8,128)(2,1)} %get-tuple-element.150) | copy-start | bytes 25165828 | tf_op jit(solution)/shard_map/while
  241.4 6.2 %copy-start.3 = (bf16[2048,2048]{1,0:T(8,128)(2,1)S(1)}, bf16[2048,2048]{1,0:T(8,128)(2,1)}, u32[]{:S(2)}) copy-start(bf16[2048,2048]{1,0:T(8,128)(2,1)} %get-tuple-element.150) | copy-start | bytes 25165828 | tf_op jit(solution)/shard_map/while
  253.4 6.2 %copy-start.3 = (bf16[2048,2048]{1,0:T(8,128)(2,1)S(1)}, bf16[2048,2048]{1,0:T(8,128)(2,1)}, u32[]{:S(2)}) copy-start(bf16[2048,2048]{1,0:T(8,128)(2,1)} %get-tuple-element.150) | copy-start | bytes 25165828 | tf_op jit(solution)/shard_map/while
  265.3 6.2 %copy-start.3 = (bf16[2048,2048]{1,0:T(8,128)(2,1)S(1)}, bf16[2048,2048]{1,0:T(8,128)(2,1)}, u32[]{:S(2)}) copy-start(bf16[2048,2048]{1,0:T(8,128)(2,1)} %get-tuple-element.150) | copy-start | bytes 25165828 | tf_op jit(solution)/shard_map/while
Sparse Core Ops, SparseCore 0:
  31.6 83.3 all-gather.2
